TPU v7x, 512 devices: a whole 4x8x8 slice. The times are simulated.
512 devices in a mesh: blk: 64 (over z_hi, y, core), seq: 4 (over x), mp: 2 (over z_lo).
Axes of the slice: x: 4, y: 8, z: 8 (z_hi: 4, z_lo: 2; z = z_hi * 2 + z_lo), core: 2. Of those that a mesh axis runs over, the one named last changes fastest.
Arguments:
- hidden: bfloat16 [8, 512, 1536], P(('mp', 'seq'), 'blk'), parts along dimension 0, may hold values from -6 to 6
- labels: int32 [4, 512], P('seq'), may hold values from 0 to 50303
- lengths: int32 [4, 8], P('seq'), may hold values from 1 to 256, 512 in all within a row
- owners: int32 [32], replicated, may hold values from 0 to 31, each once
- w_inner: bfloat16 [3072, 2, 3072], P('mp', None, 'blk'), parts along dimension 0, may hold values from -0.15625 to 0.15625
- w_bcdt: bfloat16 [3072, 304], P('mp'), parts along dimension 0, may hold values from -0.15625 to 0.15625
- conv_inner: float32 [8, 3072], P('mp', 'blk'), parts along dimension 0, may hold values from -3 to 3
- conv_bc: float32 [8, 256], P('mp'), parts along dimension 0, may hold values from -3 to 3
- dt_bias: float32 [96], P('mp'), parts along dimension 0, may hold values from -3 to 0.5
- decay_rate: float32 [96], P('mp'), parts along dimension 0, may hold values from 0.01 to 1
- d_skip: float32 [96], P('mp'), parts along dimension 0, may hold values from 0.5 to 2
- norm_gain: float32 [6144], P(('mp', 'blk')), parts along dimension 0, may hold values from 0.5 to 1.5
- w_out: bfloat16 [6144, 1536], P(('mp', 'blk')), parts along dimension 0, may hold values from -0.109375 to 0.109375
- final_gain: float32 [3072], P('mp'), parts along dimension 0, may hold values from 0.5 to 1.5
- w_head: bfloat16 [3072, 50304], P('mp', 'blk'), parts along dimension 0, may hold values from -0.33170174 to 0.33170174
Outputs:
- layer_out: bfloat16 [8, 512, 1536], P(('mp', 'seq'), 'blk'), parts along dimension 0
- token_logprob: float32 [8, 512], P(('mp', 'seq'), 'blk'), parts along dimension 0
- seq_logprob: float32 [64], P(('mp', 'seq')), parts along dimension 0
There are 2 independent parts, one for each index of `mp`. A program takes and returns all parts, laid end to end along the dimension named above; an argument that names none is the same for every part. Nothing has to cross between parts.
Inputs may be any that keep to these rules, and one draw needn't show every extreme that they name: The 8 lengths of a group sum to 512 and the longest is exactly 256. `owners`: every output slot is named once.
All inputs are finite; a program needn't handle non-finite values.
Results may differ from a plain program's by a relative error of at most 0.0055.
Values may be sent and summed in bfloat16 or wider, within the bound.
No kernel may reach another device: no remote copies, remote signals or barrier semaphores. Data moves between devices by JAX's collectives and lax.ppermute only.
A program may use at most 64 MiB of HBM per device.

v0:
```python
import jax
import jax.numpy as jnp
from jax import lax
from jax.sharding import PartitionSpec as P

D = 1536
HEADDIM = 64
NSTATE = 128
SCAN_BLOCK = 256
CONV = 4


EPSILON = 1e-05
HIGH = lax.Precision.HIGHEST


def segments_of(lengths, count):
    starts = jnp.cumsum(lengths, axis=-1) - lengths
    places = jnp.arange(count, dtype=jnp.int32)
    segment = jnp.sum((places[:, None] >= starts[None, :]).astype(jnp.int32), axis=-1) - 1
    first = jnp.take(starts, segment)
    return (segment, places - first)


def causal_conv(values, weights, position):
    total = values * weights[0]
    for shift_by in range(1, CONV):
        moved = jnp.concatenate(
            [jnp.zeros_like(values[:shift_by, :]), values[:-shift_by, :]], axis=0
        )
        total = (
            total + moved * weights[shift_by] * (position >= shift_by).astype(jnp.float32)[:, None]
        )
    return total


def final_norm(values, gain):
    widened = values.astype(jnp.float32)
    scale = lax.rsqrt(jnp.mean(widened * widened, axis=-1, keepdims=True) + EPSILON)
    return (widened * scale * gain).astype(jnp.bfloat16)


def shards(
    hidden,
    labels,
    lengths,
    owners,
    w_inner,
    w_bcdt,
    conv_inner,
    conv_bc,
    dt_bias,
    decay_rate,
    d_skip,
    norm_gain,
    w_out,
    final_gain,
    w_head,
):
    rows_own = hidden[0]
    rows_count = rows_own.shape[0]
    blk_count = lax.axis_size("blk")
    blk_index = lax.axis_index("blk")
    gathered = lax.all_gather(rows_own, "blk", axis=0, tiled=True)
    tokens_all = gathered.shape[0]
    channels = w_inner.shape[2]
    inner_total = channels * blk_count
    inner_proj = jnp.dot(
        gathered, w_inner.reshape(D, 2 * channels), preferred_element_type=jnp.float32
    ).astype(jnp.bfloat16)
    state_proj = jnp.dot(gathered, w_bcdt, preferred_element_type=jnp.float32).astype(jnp.bfloat16)
    gate_half = inner_proj[:, :channels].astype(jnp.float32)
    segment, position = segments_of(lengths[0], tokens_all)
    conv_value = jax.nn.silu(
        causal_conv(inner_proj[:, channels:].astype(jnp.float32), conv_inner, position)
    )
    conv_state = jax.nn.silu(
        causal_conv(state_proj[:, : 2 * NSTATE].astype(jnp.float32), conv_bc, position)
    )
    input_map = conv_state[:, :NSTATE]
    output_map = conv_state[:, NSTATE:]
    step_size = jax.nn.softplus(state_proj[:, 2 * NSTATE :].astype(jnp.float32) + dt_bias)
    log_heads = -(step_size * decay_rate)
    first_channel = blk_index * channels
    channel_head = (first_channel + jnp.arange(channels, dtype=jnp.int32)) // HEADDIM
    head_low = first_channel // HEADDIM
    head_high = (first_channel + channels - 1) // HEADDIM
    mask_high = (channel_head == head_high).astype(jnp.float32)
    mask_low = 1.0 - mask_high
    step_pair = jnp.concatenate(
        [
            lax.dynamic_slice_in_dim(step_size, head_low, 1, 1),
            lax.dynamic_slice_in_dim(step_size, head_high, 1, 1),
        ],
        axis=1,
    )
    log_pair = jnp.concatenate(
        [
            lax.dynamic_slice_in_dim(log_heads, head_low, 1, 1),
            lax.dynamic_slice_in_dim(log_heads, head_high, 1, 1),
        ],
        axis=1,
    )
    step_channel = step_pair[:, 0:1] * mask_low + step_pair[:, 1:2] * mask_high
    driven = conv_value * step_channel
    slot_masks = (mask_low, mask_high)
    blocks = tokens_all // SCAN_BLOCK
    order = jnp.arange(SCAN_BLOCK, dtype=jnp.int32)
    causal = order[:, None] >= order[None, :]

    def block_step(carry, inputs):
        carried, previous = carry
        drive_block, in_block, out_block, log_block, seg_block = inputs
        cumulative = jnp.cumsum(log_block, axis=0)
        gram = jnp.dot(out_block, in_block.T, precision=HIGH)
        same = (seg_block[:, None] == seg_block[None, :]) & causal
        result = jnp.zeros((SCAN_BLOCK, channels), jnp.float32)
        for slot_index in range(2):
            column = cumulative[:, slot_index]
            spread = jnp.minimum(column[:, None] - column[None, :], 0.0)
            weights = jnp.where(same, jnp.exp(spread), 0.0)
            result = result + jnp.dot(
                gram * weights, drive_block * slot_masks[slot_index], precision=HIGH
            )
        carried_in = carried * (seg_block[0] == previous).astype(jnp.float32)
        rising = jnp.exp(cumulative[:, 0:1]) * mask_low + jnp.exp(cumulative[:, 1:2]) * mask_high
        leading = (seg_block == seg_block[0]).astype(jnp.float32)[:, None]
        result = result + leading * rising * jnp.dot(out_block, carried_in.T, precision=HIGH)
        trailing = (seg_block == seg_block[-1]).astype(jnp.float32)[:, None]
        tail_low = jnp.exp(cumulative[-1:, 0:1] - cumulative[:, 0:1])
        tail_high = jnp.exp(cumulative[-1:, 1:2] - cumulative[:, 1:2])
        tail = tail_low * mask_low + tail_high * mask_high
        whole_block = (seg_block[-1] == seg_block[0]).astype(jnp.float32)
        carried_new = whole_block * rising[-1][:, None] * carried_in + jnp.dot(
            (drive_block * tail * trailing).T, in_block, precision=HIGH
        )
        return ((carried_new, seg_block[-1]), result)

    initial = (jnp.zeros((channels, NSTATE), jnp.float32), jnp.int32(-1))
    scan_inputs = (
        driven.reshape(blocks, SCAN_BLOCK, channels),
        input_map.reshape(blocks, SCAN_BLOCK, NSTATE),
        output_map.reshape(blocks, SCAN_BLOCK, NSTATE),
        log_pair.reshape(blocks, SCAN_BLOCK, 2),
        segment.reshape(blocks, SCAN_BLOCK),
    )
    final_carry, scanned = lax.scan(block_step, initial, scan_inputs)
    mixed = scanned.reshape(tokens_all, channels) + jnp.take(d_skip, channel_head) * conv_value
    gated = mixed * jax.nn.silu(gate_half)
    squares = lax.psum(jnp.sum(gated * gated, axis=1), "blk")
    inverse = lax.rsqrt(squares / inner_total + EPSILON)
    gated_norm = (gated * inverse[:, None] * norm_gain).astype(jnp.bfloat16)
    delta_own = lax.psum_scatter(
        jnp.dot(gated_norm, w_out, preferred_element_type=jnp.float32),
        "blk",
        scatter_dimension=0,
        tiled=True,
    )
    layer_own = (rows_own.astype(jnp.float32) + delta_own).astype(jnp.bfloat16)
    logits = jnp.dot(
        lax.all_gather(final_norm(layer_own, final_gain), "blk", axis=0, tiled=True),
        w_head,
        preferred_element_type=jnp.float32,
    )
    vocab_local = w_head.shape[1]
    local_label = labels[0] - blk_index * vocab_local
    hit = jnp.arange(vocab_local, dtype=jnp.int32)[None, :] == local_label[:, None]
    target_local = jnp.sum(jnp.where(hit, logits, 0.0), axis=1)
    top_local = jnp.max(logits, axis=1)
    top_all = lax.pmax(top_local, "blk")
    expsum_local = jnp.sum(jnp.exp(logits - top_all[:, None]), axis=1)
    expsum_all, target_all = lax.psum((expsum_local, target_local), "blk")
    logprob = target_all - (top_all + jnp.log(expsum_all))
    token_own = lax.dynamic_slice_in_dim(logprob, blk_index * rows_count, rows_count, 0)
    seqs_count = lengths.shape[1]
    onehot = (segment[:, None] == jnp.arange(seqs_count, dtype=jnp.int32)[None, :]).astype(
        jnp.float32
    )
    sums = jnp.dot(logprob, onehot, precision=HIGH)
    seq_index = lax.axis_index("seq")
    mine = lax.dynamic_slice_in_dim(owners, seq_index * seqs_count, seqs_count, 0)
    placement = (mine[:, None] == jnp.arange(owners.shape[0], dtype=jnp.int32)[None, :]).astype(
        jnp.float32
    )
    spread_sums = jnp.dot(sums, placement, precision=HIGH)
    seq_own = lax.psum_scatter(spread_sums, "seq", scatter_dimension=0, tiled=True)
    return (layer_own[None], token_own[None], seq_own)


def solution(mesh):
    in_specs = (
        P(("mp", "seq"), "blk", None),
        P("seq", None),
        P("seq", None),
        P(),
        P("mp", None, "blk"),
        P("mp", None),
        P("mp", "blk"),
        P("mp", None),
        P("mp"),
        P("mp"),
        P("mp"),
        P(("mp", "blk")),
        P(("mp", "blk"), None),
        P("mp"),
        P("mp", "blk"),
    )
    out_specs = (P(("mp", "seq"), "blk", None), P(("mp", "seq"), "blk"), P(("mp", "seq")))
    return jax.shard_map(shards, mesh=mesh, in_specs=in_specs, out_specs=out_specs, check_vma=False)
```

profile of v0, /device:TPU:1, one launch (start us, length us, event | category | flops | bytes accessed | tf_op | source)
XLA Modules:
  0.0 819.6 jit_solution(5413940078656478816)
XLA Ops:
  10.2 1.4 gather_fusion
  13.6 1.4 slice_bitcast_fusion.3
  15.0 4.4 compare_select_fusion.5
  21.0 80.3 %all-gather.6.cloned.1.call-done = bf16[1,512,1536]{2,1,0:T(8,128)(2,1)} async-done(((bf16[1,8,1536]{2,1,0:T(8,128)(2,1)}), bf16[1,512,1536]{2,1,0:T(8,128)(2,1)}) %all-gather.6.cloned.1.call-update) | async-done | bytes 1572880 | tf_op jit(solution)/shard_map/all_gather | solution.py:64
  101.3 2.3 fusion.71
  104.8 2.0 fusion.74
  108.1 29.1 %while.17 = (s32[]{:T(128)}, f32[48,128]{1,0:T(8,128)S(1)}, s32[]{:T(128)}, f32[2,256,48]{1,0,2:T(2,128)}, s32[2,256]{1,0:T(2,128)}, /*index=5*/f32[2,256,2]{1,2...) while((s32[]{:T(128)}, f32[48,128]{1,0:T(8,128)S(1)}, ...), condition=%wide.region_5.6_spmd.clone.clone.clone, body=%wide.region_2.5_spmd.clone.clone.clone.sunk | while | flops 215140816 | bytes 2177448 | solution.py:147
  113.8 1.3 constant_dynamic-slice_fusion.12
  115.1 1.9 compare_convert_fusion.10
  118.0 2.2 dynamic_update_slice.8
  125.0 1.3 fusion.130
  128.4 1.3 constant_dynamic-slice_fusion.12
  129.6 1.9 compare_convert_fusion.10
  132.5 2.2 dynamic_update_slice.8
  138.8 138.1 %psum.21 = f32[512]{0:T(512)S(1)} all-reduce(f32[512]{0:T(512)S(1)} %get-tuple-element.251), channel_id=1, replica_groups=mesh['blk'=64,'seq'=4,'mp'=2] {'blk'}, use_global_device_ids=true, to_apply=%region_7.8 | all-reduce | flops 512 | bytes 4096 | tf_op jit(solution)/shard_map/psum | solution.py:150
  276.9 3.0 fusion.85
  279.9 148.0 %reduce-scatter.2.cloned.1.call-done = f32[8,1536]{1,0:T(8,128)} async-done(((f32[512,1536]{1,0:T(8,128)}), f32[8,1536]{1,0:T(8,128)}) %reduce-scatter.2.cloned.1.call-update) | async-done | bytes 49168 | tf_op jit(solution)/shard_map/reduce_scatter | solution.py:153
  429.7 1.3 dynamic-slice
  431.7 85.4 %all-gather.4.cloned.1.call-done = bf16[512,1536]{1,0:T(8,128)(2,1)} async-done(((bf16[8,1536]{1,0:T(8,128)(2,1)}), bf16[512,1536]{1,0:T(8,128)(2,1)}) %all-gather.4.cloned.1.call-update) | async-done | bytes 1572880 | tf_op jit(solution)/shard_map/all_gather | solution.py:161
  517.1 4.0 fusion.101
  521.1 138.1 %pmax.7 = f32[512]{0:T(512)S(1)} all-reduce(f32[512]{0:T(512)S(1)} %get-tuple-element.299), channel_id=1, replica_groups=mesh['blk'=64,'seq'=4,'mp'=2] {'blk'}, use_global_device_ids=true, to_apply=%region_13.14 | all-reduce | flops 512 | bytes 4096 | tf_op jit(solution)/shard_map/pmax | solution.py:170
  659.2 1.9 exponential_reduce_fusion
  661.1 142.0 %all-reduce.7 = (f32[512]{0:T(512)S(1)}, f32[512]{0:T(512)S(1)}) all-reduce(f32[512]{0:T(512)S(1)} %get-tuple-element.222, f32[512]{0:T(512)S(1)} %get-tuple-element.221), channel_id=1, replica_groups=mesh['blk'=64,'seq'=4,'mp'=2] {'blk'}, use_global_device_ids=true, to_apply=%region_11.12 | all-reduce | flops 1024 | bytes 8192 | tf_op jit(solution)/shard_map/psum | solution.py:172
  803.6 8.4 %all-reduce.6 = f32[32]{0:T(128)S(1)} all-reduce(f32[32]{0:T(128)S(1)} %convolution_bitcast_fusion.1), channel_id=4, replica_groups=mesh['blk'=64,'seq'=4,'mp'=2] {'seq'}, use_global_device_ids=true, to_apply=%region_16.17.clone | all-reduce | flops 32 | bytes 256
  (135 shorter events, 25.4 us)
Async XLA Ops:
  7.2 509.9 %copy-start = (bf16[1536,786]{0,1:T(8,128)(2,1)S(1)}, bf16[1536,786]{0,1:T(8,128)(2,1)}, u32[]{:S(2)}) copy-start(bf16[1536,786]{0,1:T(8,128)(2,1)} %param.31) | copy-start | bytes 7243780
  7.2 94.1 %all-gather.6.cloned.1.call-start = ((), (), s32[]{:S(2)}) async-start(), calls=%async_computation.3 | async-start | bytes 1597440 | tf_op jit(solution)/shard_map/all_gather | solution.py:64
  7.9 420.1 %reduce-scatter.2.cloned.1.call-start = ((), (), s32[]{:S(2)}) async-start(), calls=%async_computation.1 | async-start | bytes 3194880 | tf_op jit(solution)/shard_map/reduce_scatter | solution.py:153
  9.6 94.1 %copy-start.5 = (s32[512]{0:T(512)}, s32[512]{0:T(512)S(1)}, u32[]{:S(2)}) copy-start(s32[512]{0:T(512)S(1)} %get-tuple-element.290) | copy-start | bytes 6148
  20.1 83.6 %copy-start.11 = (f32[512]{0:T(512)}, f32[512]{0:T(512)S(1)}, u32[]{:S(2)}) copy-start(f32[512]{0:T(512)S(1)} %get-tuple-element.257) | copy-start | bytes 6148
  20.1 83.6 %copy-start.7 = (f32[512]{0:T(512)}, f32[512]{0:T(512)S(1)}, u32[]{:S(2)}) copy-start(f32[512]{0:T(512)S(1)} %get-tuple-element.287) | copy-start | bytes 6148
  20.1 83.6 %copy-start.9 = (f32[512]{0:T(512)}, f32[512]{0:T(512)S(1)}, u32[]{:S(2)}) copy-start(f32[512]{0:T(512)S(1)} %get-tuple-element.288) | copy-start | bytes 6148
  104.7 2.3 copy-start.8
  104.7 2.3 copy-start.10
  104.8 2.3 copy-start.12
  104.8 2.3 copy-start.15
  104.8 2.3 copy-start.16
  104.8 2.3 copy-start.17
  104.8 2.3 copy-start.18
  104.8 2.3 copy-start.19
  104.8 2.3 copy-start.20
  108.1 168.8 %copy-start.1 = (bf16[48,1536]{1,0:T(8,128)(2,1)S(1)}, bf16[48,1536]{1,0:T(8,128)(2,1)}, u32[]{:S(2)}) copy-start(bf16[48,1536]{1,0:T(8,128)(2,1)} %param.29) | copy-start | bytes 442372
  279.9 148.1 %copy-start.4 = (bf16[1,8,1536]{2,1,0:T(8,128)(2,1)S(1)}, bf16[1,8,1536]{2,1,0:T(8,128)(2,1)}, u32[]{:S(2)}) copy-start(bf16[1,8,1536]{2,1,0:T(8,128)(2,1)} %param.17) | copy-start | bytes 73732
  279.9 149.1 %copy-start.13 = (f32[1536]{0:T(1024)S(1)}, f32[1536]{0:T(1024)}, u32[]{:S(2)}) copy-start(f32[1536]{0:T(1024)} %param.30) | copy-start | bytes 18436
  279.9 149.8 %copy-start.23 = (s32[32]{0:T(128)S(1)}, s32[32]{0:T(128)}, u32[]{:S(2)}) copy-start(s32[32]{0:T(128)} %param.20) | copy-start | bytes 388
  279.9 151.8 %copy-start.14 = (s32[1,512]{1,0:T(1,128)S(1)}, s32[1,512]{1,0:T(1,128)}, u32[]{:S(2)}) copy-start(s32[1,512]{1,0:T(1,128)} %param.18) | copy-start | bytes 6148
  279.9 237.2 %all-gather.4.cloned.1.call-start = ((), (), s32[]{:S(2)}) async-start(), calls=%async_computation.2 | async-start | bytes 1597440 | tf_op jit(solution)/shard_map/all_gather | solution.py:161
  428.9 92.2 %copy-start.3 = (bf16[8,1536]{1,0:T(8,128)(2,1)}, bf16[8,1536]{1,0:T(8,128)(2,1)S(1)}, u32[]{:S(2)}) copy-start(bf16[8,1536]{1,0:T(8,128)(2,1)S(1)} %get-tuple-element.250) | copy-start | bytes 73732
  521.1 282.0 %copy-start.6 = (s32[512]{0:T(512)S(1)}, s32[512]{0:T(512)}, u32[]{:S(2)}) copy-start(s32[512]{0:T(512)} %copy-done.5) | copy-start | bytes 6148
  (4 other events, 6.4 us)
Sparse Core Ops, SparseCore 0:
  11.3 89.9 all-gather.5
  280.0 147.9 reduce-scatter.1
  431.3 85.7 all-gather.3
where the time goes:
time: 821 us; the launch traced here: 820 us
  blocking collectives  427 us (52%)
  waiting for transfers between devices  314 us (38%)
  other arithmetic  22.4 us (3%)
  local copies, waits for them, and re-layouts  20.4 us (2%)
  matrix products  15.5 us (2%)
  between operations  14.9 us (2%)
    reduce_scatter x1, waiting for transfers between devices, shards(): lax.psum_scatter(jnp.dot(gated_norm, w_out, preferred_element_type=jnp.fl...  148 us
    psum x1, blocking collectives, shards(): expsum_all, target_all = lax.psum((expsum_local, target_local), 'blk')  142 us
    psum x1, blocking collectives, shards(): squares = lax.psum(jnp.sum(gated * gated, axis=1), 'blk')  138 us
    pmax x1, blocking collectives, shards(): top_all = lax.pmax(top_local, 'blk')  138 us
    all_gather x1, waiting for transfers between devices, shards(): lax.all_gather(final_norm(layer_own, final_gain), 'blk', axis=0, tiled=True)  85.4 us
    all_gather x1, waiting for transfers between devices, shards(): gathered = lax.all_gather(rows_own, 'blk', axis=0, tiled=True)  80.3 us
  transfers between devices with their start and end apart: 3, of which 3 were waited for; matrix products, arithmetic and copies ran while one was open for 2% of the time, Pallas kernels for 0%

commit v1 on v0

--- a/solution.py
+++ b/solution.py
@@ -1,6 +1,7 @@
 import jax
 import jax.numpy as jnp
 from jax import lax
+from jax.sharding import Mesh
 from jax.sharding import PartitionSpec as P
 
 D = 1536
@@ -12,6 +13,32 @@
 
 EPSILON = 1e-05
 HIGH = lax.Precision.HIGHEST
+BLK = ("bz", "by", "bc")
+
+
+def gather_rows(rows):
+    part = lax.all_gather(rows, "bz", axis=0)
+    part = lax.all_gather(part, "by", axis=1)
+    part = lax.all_gather(part, "bc", axis=2)
+    return part.reshape((-1,) + rows.shape[1:])
+
+
+def scatter_rows(values):
+    bz = lax.axis_size("bz")
+    by = lax.axis_size("by")
+    bc = lax.axis_size("bc")
+    part = values.reshape((bz, by, bc, -1) + values.shape[1:])
+    part = lax.psum_scatter(part, "bc", scatter_dimension=2)
+    part = lax.psum_scatter(part, "by", scatter_dimension=1)
+    return lax.psum_scatter(part, "bz", scatter_dimension=0)
+
+
+def sum_blk(values):
+    return lax.psum(lax.psum(lax.psum(values, "bc"), "by"), "bz")
+
+
+def max_blk(values):
+    return lax.pmax(lax.pmax(lax.pmax(values, "bc"), "by"), "bz")
 
 
 def segments_of(lengths, count):
@@ -59,9 +86,11 @@
 ):
     rows_own = hidden[0]
     rows_count = rows_own.shape[0]
-    blk_count = lax.axis_size("blk")
-    blk_index = lax.axis_index("blk")
-    gathered = lax.all_gather(rows_own, "blk", axis=0, tiled=True)
+    blk_count = lax.axis_size("bz") * lax.axis_size("by") * lax.axis_size("bc")
+    blk_index = (
+        lax.axis_index("bz") * lax.axis_size("by") + lax.axis_index("by")
+    ) * lax.axis_size("bc") + lax.axis_index("bc")
+    gathered = gather_rows(rows_own)
     tokens_all = gathered.shape[0]
     channels = w_inner.shape[2]
     inner_total = channels * blk_count
@@ -147,18 +176,13 @@
     final_carry, scanned = lax.scan(block_step, initial, scan_inputs)
     mixed = scanned.reshape(tokens_all, channels) + jnp.take(d_skip, channel_head) * conv_value
     gated = mixed * jax.nn.silu(gate_half)
-    squares = lax.psum(jnp.sum(gated * gated, axis=1), "blk")
+    squares = sum_blk(jnp.sum(gated * gated, axis=1))
     inverse = lax.rsqrt(squares / inner_total + EPSILON)
     gated_norm = (gated * inverse[:, None] * norm_gain).astype(jnp.bfloat16)
-    delta_own = lax.psum_scatter(
-        jnp.dot(gated_norm, w_out, preferred_element_type=jnp.float32),
-        "blk",
-        scatter_dimension=0,
-        tiled=True,
-    )
+    delta_own = scatter_rows(jnp.dot(gated_norm, w_out, preferred_element_type=jnp.float32))
     layer_own = (rows_own.astype(jnp.float32) + delta_own).astype(jnp.bfloat16)
     logits = jnp.dot(
-        lax.all_gather(final_norm(layer_own, final_gain), "blk", axis=0, tiled=True),
+        gather_rows(final_norm(layer_own, final_gain)),
         w_head,
         preferred_element_type=jnp.float32,
     )
@@ -167,9 +191,9 @@
     hit = jnp.arange(vocab_local, dtype=jnp.int32)[None, :] == local_label[:, None]
     target_local = jnp.sum(jnp.where(hit, logits, 0.0), axis=1)
     top_local = jnp.max(logits, axis=1)
-    top_all = lax.pmax(top_local, "blk")
+    top_all = max_blk(top_local)
     expsum_local = jnp.sum(jnp.exp(logits - top_all[:, None]), axis=1)
-    expsum_all, target_all = lax.psum((expsum_local, target_local), "blk")
+    expsum_all, target_all = sum_blk((expsum_local, target_local))
     logprob = target_all - (top_all + jnp.log(expsum_all))
     token_own = lax.dynamic_slice_in_dim(logprob, blk_index * rows_count, rows_count, 0)
     seqs_count = lengths.shape[1]
@@ -188,22 +212,25 @@
 
 
 def solution(mesh):
+    blk = mesh.shape["blk"]
+    split = mesh.devices.reshape((blk // 16, 8, 2) + mesh.devices.shape[1:])
+    mesh = Mesh(split, BLK + mesh.axis_names[1:])
     in_specs = (
-        P(("mp", "seq"), "blk", None),
+        P(("mp", "seq"), BLK, None),
         P("seq", None),
         P("seq", None),
         P(),
-        P("mp", None, "blk"),
+        P("mp", None, BLK),
         P("mp", None),
-        P("mp", "blk"),
+        P("mp", BLK),
         P("mp", None),
         P("mp"),
         P("mp"),
         P("mp"),
-        P(("mp", "blk")),
-        P(("mp", "blk"), None),
-        P("mp"),
-        P("mp", "blk"),
-    )
-    out_specs = (P(("mp", "seq"), "blk", None), P(("mp", "seq"), "blk"), P(("mp", "seq")))
+        P(("mp",) + BLK),
+        P(("mp",) + BLK, None),
+        P("mp"),
+        P("mp", BLK),
+    )
+    out_specs = (P(("mp", "seq"), BLK, None), P(("mp", "seq"), BLK), P(("mp", "seq")))
     return jax.shard_map(shards, mesh=mesh, in_specs=in_specs, out_specs=out_specs, check_vma=False)

time: 821 us -> 384 us (0.47)
  the two profiles are of different devices: /device:TPU:1 before, /device:TPU:8 now
where the time goes in v1:
time: 384 us; the launch traced here: 383 us
  blocking collectives  193 us (50%)
  waiting for transfers between devices  115 us (30%)
  local copies, waits for them, and re-layouts  20 us (5%)
  other arithmetic  20 us (5%)
  between operations  15 us (4%)
  matrix products  13.9 us (4%)
  loops' own time  5.31 us (1%)
    psum x6, blocking collectives, sum_blk(): return lax.psum(lax.psum(lax.psum(values, 'bc'), 'by'), 'bz')  60.5 us
    all_gather x2, blocking collectives, gather_rows(): part = lax.all_gather(part, 'by', axis=1)  57.1 us
    reduce_scatter x1, waiting for transfers between devices, scatter_rows(): part = lax.psum_scatter(part, 'by', scatter_dimension=1)  46.6 us
    all_gather x2, blocking collectives, gather_rows(): part = lax.all_gather(rows, 'bz', axis=0)  33.5 us
    pmax x3, blocking collectives, max_blk(): return lax.pmax(lax.pmax(lax.pmax(values, 'bc'), 'by'), 'bz')  31.4 us
    reduce_scatter x1, waiting for transfers between devices, scatter_rows(): return lax.psum_scatter(part, 'bz', scatter_dimension=0)  31.1 us
    all_gather x2, waiting for transfers between devices, gather_rows(): part = lax.all_gather(part, 'bc', axis=2)  21.4 us
    reduce_scatter x1, waiting for transfers between devices, scatter_rows(): part = lax.psum_scatter(part, 'bc', scatter_dimension=2)  16.1 us
  transfers between devices with their start and end apart: 5, of which 5 were waited for; matrix products, arithmetic and copies ran while one was open for 3% of the time, Pallas kernels for 0%

profile of v1, /device:TPU:8, one launch (start us, length us, event | category | flops | bytes accessed | tf_op | source)
XLA Modules:
  0.0 382.6 jit_solution(8518555790015400098)
XLA Ops:
  7.3 19.6 %all_gather.31 = bf16[4,8,1536]{2,1,0:T(8,128)(2,1)S(1)} all-gather(bf16[1,8,1536]{2,1,0:T(8,128)(2,1)} %param.17), channel_id=1, replica_groups=mesh['bz'=4,'by'=8,'bc'=2,'seq'=4,'mp'=2] {'bz'}, dimensions={0}, use_global_device_ids=true | all-gather | bytes 122880 | tf_op jit(solution)/shard_map/all_gather | solution.py:20
  26.9 28.9 %all-gather = bf16[4,64,1536]{2,1,0:T(8,128)(2,1)} all-gather(bf16[4,8,1536]{2,1,0:T(8,128)(2,1)S(1)} %all_gather.31), channel_id=2, replica_groups=mesh['bz'=4,'by'=8,'bc'=2,'seq'=4,'mp'=2] {'by'}, dimensions={1}, use_global_device_ids=true | all-gather | bytes 884736 | tf_op jit(solution)/shard_map/all_gather | solution.py:21
  59.4 4.5 %compare_select_fusion.5 = s32[512,1]{0,1:T(1,128)S(1)} fusion(s32[]{:T(128)} %bitcast.14, s32[]{:T(128)} %bitcast.15, s32[]{:T(128)} %bitcast.16, s32[]{:T(128)} %bitcast.17, s32[]{:T(128)} %bitcast.18, s32[]{:T(128)} %bitcast.20, s32[]{:T(128)} %bitcast.19, s32[512,1]{0,1:T(1,128)S(1)} %bitcast.207, s32[512,1]{0,1:T(1,128)S(1)} %bitcast.203), kind=kLoop, calls=%fused_computation.128 | loop fusion | flops 7168 | bytes 6172 | tf_op jit(solution)/shard_map/jit(_take)/gather | solution.py:48
  64.6 7.7 %all-gather.7.cloned.1.call-done = bf16[4,8,16,1536]{3,2,1,0:T(8,128)(2,1)} async-done(((bf16[4,8,8,1536]{3,2,1,0:T(8,128)(2,1)}), bf16[4,8,16,1536]{3,2,1,0:T(8,128)(2,1)}) %all-gather.7.cloned.1.call-update) | async-done | bytes 1572880 | tf_op jit(solution)/shard_map/all_gather | solution.py:22
  72.4 2.3 convolution_convert_fusion
  79.1 29.2 %while.17 = (s32[]{:T(128)}, f32[48,128]{1,0:T(8,128)S(1)}, s32[]{:T(128)}, f32[2,256,48]{1,0,2:T(2,128)}, s32[2,256]{1,0:T(2,128)}, /*index=5*/f32[2,256,2]{1,2...) while((s32[]{:T(128)}, f32[48,128]{1,0:T(8,128)S(1)}, ...), condition=%wide.region_5.6_spmd.clone.clone.clone, body=%wide.region_2.5_spmd.clone.clone.clone.sunk | while | flops 215140816 | bytes 2177448 | solution.py:176
  89.1 2.2 dynamic_update_slice.8
  110.0 2.5 psum.63
  112.4 15.7 %psum.64 = f32[512]{0:T(512)S(1)} all-reduce(f32[512]{0:T(512)S(1)} %psum.63), channel_id=1, replica_groups=mesh['bz'=4,'by'=8,'bc'=2,'seq'=4,'mp'=2] {'by'}, use_global_device_ids=true, to_apply=%region_8.9 | all-reduce | flops 512 | bytes 4096 | tf_op jit(solution)/shard_map/psum | solution.py:37
  128.1 13.3 %psum.65 = f32[512]{0:T(512)S(1)} all-reduce(f32[512]{0:T(512)S(1)} %psum.64), channel_id=1, replica_groups=mesh['bz'=4,'by'=8,'bc'=2,'seq'=4,'mp'=2] {'bz'}, use_global_device_ids=true, to_apply=%region_9.10 | all-reduce | flops 512 | bytes 4096 | tf_op jit(solution)/shard_map/psum | solution.py:37
  144.7 16.1 %reduce-scatter.4.cloned.1.call-done = f32[4,8,1,8,1536]{4,3,0,1,2:T(8,128)} async-done(((f32[4,8,2,8,1536]{4,3,0,1,2:T(8,128)}), f32[4,8,1,8,1536]{4,3,0,1,2:T(8,128)}) %reduce-scatter.4.cloned.1.call-update) | async-done | bytes 1572880 | tf_op jit(solution)/shard_map/reduce_scatter | solution.py:31
  160.9 46.6 %reduce-scatter.6.cloned.1.call-done = f32[4,1,8,1536]{3,2,0,1:T(8,128)} async-done(((f32[4,8,8,1536]{3,2,0,1:T(8,128)}), f32[4,1,8,1536]{3,2,0,1:T(8,128)}) %reduce-scatter.6.cloned.1.call-update) | async-done | bytes 196624 | tf_op jit(solution)/shard_map/reduce_scatter | solution.py:32
  207.6 31.1 %reduce-scatter.8.cloned.1.call-done = f32[1,8,1536]{2,1,0:T(8,128)} async-done(((f32[4,8,1536]{2,1,0:T(8,128)}), f32[1,8,1536]{2,1,0:T(8,128)}) %reduce-scatter.8.cloned.1.call-update) | async-done | bytes 49168 | tf_op jit(solution)/shard_map/reduce_scatter | solution.py:33
  239.7 13.9 %all_gather.36 = bf16[4,8,1536]{2,1,0:T(8,128)(2,1)S(1)} all-gather(bf16[1,8,1536]{2,1,0:T(8,128)(2,1)S(1)} %fusion.73), channel_id=1, replica_groups=mesh['bz'=4,'by'=8,'bc'=2,'seq'=4,'mp'=2] {'bz'}, dimensions={0}, use_global_device_ids=true | all-gather | bytes 122880 | tf_op jit(solution)/shard_map/all_gather | solution.py:20
  253.6 28.3 %all-gather.2 = bf16[4,64,1536]{2,1,0:T(8,128)(2,1)} all-gather(bf16[4,8,1536]{2,1,0:T(8,128)(2,1)S(1)} %all_gather.36), channel_id=4, replica_groups=mesh['bz'=4,'by'=8,'bc'=2,'seq'=4,'mp'=2] {'by'}, dimensions={1}, use_global_device_ids=true | all-gather | bytes 884736 | tf_op jit(solution)/shard_map/all_gather | solution.py:21
  284.0 13.7 %all-gather.9.cloned.1.call-done = bf16[4,8,16,1536]{3,2,1,0:T(8,128)(2,1)} async-done(((bf16[4,8,8,1536]{3,2,1,0:T(8,128)(2,1)}), bf16[4,8,16,1536]{3,2,1,0:T(8,128)(2,1)}) %all-gather.9.cloned.1.call-update) | async-done | bytes 1572880 | tf_op jit(solution)/shard_map/all_gather | solution.py:22
  297.7 4.1 %fusion.89 = (f32[512]{0:T(512)S(1)}, f32[512,786]{0,1:T(8,128)}) fusion(bf16[512,1536]{1,0:T(8,128)(2,1)} %bitcast.217, bf16[1536,786]{0,1:T(8,128)(2,1)S(1)} %copy-done), kind=kOutput, calls=%fused_computation.181 | convolution fusion | flops 1236673024 | bytes 5599232 | tf_op jit(solution)/shard_map/dot_general | solution.py:184
  301.7 2.4 pmax.21
  304.2 15.7 %pmax.22 = f32[512]{0:T(512)S(1)} all-reduce(f32[512]{0:T(512)S(1)} %pmax.21), channel_id=1, replica_groups=mesh['bz'=4,'by'=8,'bc'=2,'seq'=4,'mp'=2] {'by'}, use_global_device_ids=true, to_apply=%region_20.21 | all-reduce | flops 512 | bytes 4096 | tf_op jit(solution)/shard_map/pmax | solution.py:41
  319.9 13.3 %pmax.23 = f32[512]{0:T(512)S(1)} all-reduce(f32[512]{0:T(512)S(1)} %pmax.22), channel_id=1, replica_groups=mesh['bz'=4,'by'=8,'bc'=2,'seq'=4,'mp'=2] {'bz'}, use_global_device_ids=true, to_apply=%region_21.22 | all-reduce | flops 512 | bytes 4096 | tf_op jit(solution)/shard_map/pmax | solution.py:41
  335.0 2.5 all-reduce.9
  337.5 15.9 %all-reduce.7 = (f32[512]{0:T(512)S(1)}, f32[512]{0:T(512)S(1)}) all-reduce(f32[512]{0:T(512)S(1)} %get-tuple-element.249, f32[512]{0:T(512)S(1)} %get-tuple-element.250), channel_id=1, replica_groups=mesh['bz'=4,'by'=8,'bc'=2,'seq'=4,'mp'=2] {'by'}, use_global_device_ids=true, to_apply=%region_16.17 | all-reduce | flops 1024 | bytes 8192 | tf_op jit(solution)/shard_map/psum | solution.py:37
  353.4 10.6 %all-reduce.8 = (f32[512]{0:T(512)S(1)}, f32[512]{0:T(512)S(1)}) all-reduce(f32[512]{0:T(512)S(1)} %get-tuple-element.245, f32[512]{0:T(512)S(1)} %get-tuple-element.246), channel_id=1, replica_groups=mesh['bz'=4,'by'=8,'bc'=2,'seq'=4,'mp'=2] {'bz'}, use_global_device_ids=true, to_apply=%region_17.18 | all-reduce | flops 1024 | bytes 8192 | tf_op jit(solution)/shard_map/psum | solution.py:37
  364.5 10.4 %all-reduce.6 = f32[32]{0:T(128)S(1)} all-reduce(f32[32]{0:T(128)S(1)} %convolution_bitcast_fusion.1), channel_id=9, replica_groups=mesh['bz'=4,'by'=8,'bc'=2,'seq'=4,'mp'=2] {'seq'}, use_global_device_ids=true, to_apply=%region_26.27.clone | all-reduce | flops 32 | bytes 256
  (160 shorter events, 41.0 us)
Async XLA Ops:
  7.2 290.5 %copy-start = (bf16[1536,786]{0,1:T(8,128)(2,1)S(1)}, bf16[1536,786]{0,1:T(8,128)(2,1)}, u32[]{:S(2)}) copy-start(bf16[1536,786]{0,1:T(8,128)(2,1)} %param.31) | copy-start | bytes 7243780
  7.2 48.6 %copy-start.26 = (s32[1,8]{1,0:T(1,128)S(1)}, s32[1,8]{1,0:T(1,128)}, u32[]{:S(2)}) copy-start(s32[1,8]{1,0:T(1,128)} %param.19) | copy-start | bytes 100
  7.2 49.6 %copy-start.1 = (f32[48]{0:T(128)S(1)}, f32[48]{0:T(128)}, u32[]{:S(2)}) copy-start(f32[48]{0:T(128)} %param.27) | copy-start | bytes 580
  7.2 51.6 %copy-start.16 = (f32[4,48]{1,0:T(4,128)S(1)}, f32[4,48]{1,0:T(4,128)}, u32[]{:S(2)}) copy-start(f32[4,48]{1,0:T(4,128)} %param.23) | copy-start | bytes 2308
  7.2 57.4 %copy-start.15 = (f32[4,256]{1,0:T(4,128)S(1)}, f32[4,256]{1,0:T(4,128)}, u32[]{:S(2)}) copy-start(f32[4,256]{1,0:T(4,128)} %param.24) | copy-start | bytes 12292
  7.2 65.2 %all-gather.7.cloned.1.call-start = ((), (), s32[]{:S(2)}) async-start(), calls=%async_computation.6 | async-start | bytes 2359296 | tf_op jit(solution)/shard_map/all_gather | solution.py:22
  55.8 105.1 %reduce-scatter.4.cloned.1.call-start = ((), (), s32[]{:S(2)}) async-start(), calls=%async_computation.3 | async-start | bytes 4718592 | tf_op jit(solution)/shard_map/reduce_scatter | solution.py:31
  56.1 18.6 %copy-start.6 = (s32[512]{0:T(512)}, s32[512]{0:T(512)S(1)}, u32[]{:S(2)}) copy-start(s32[512]{0:T(512)S(1)} %get-tuple-element.294) | copy-start | bytes 6148
  64.6 10.2 %copy-start.12 = (f32[512]{0:T(512)}, f32[512]{0:T(512)S(1)}, u32[]{:S(2)}) copy-start(f32[512]{0:T(512)S(1)} %get-tuple-element.261) | copy-start | bytes 6148
  64.6 10.2 %copy-start.8 = (f32[512]{0:T(512)}, f32[512]{0:T(512)S(1)}, u32[]{:S(2)}) copy-start(f32[512]{0:T(512)S(1)} %get-tuple-element.291) | copy-start | bytes 6148
  64.6 10.2 %copy-start.10 = (f32[512]{0:T(512)}, f32[512]{0:T(512)S(1)}, u32[]{:S(2)}) copy-start(f32[512]{0:T(512)S(1)} %get-tuple-element.292) | copy-start | bytes 6148
  75.8 2.3 copy-start.9
  75.8 2.3 copy-start.11
  75.8 2.3 copy-start.13
  79.1 62.3 %copy-start.2 = (bf16[48,1536]{1,0:T(8,128)(2,1)S(1)}, bf16[48,1536]{1,0:T(8,128)(2,1)}, u32[]{:S(2)}) copy-start(bf16[48,1536]{1,0:T(8,128)(2,1)} %param.29) | copy-start | bytes 442372
  144.7 94.0 %copy-start.5 = (bf16[1,8,1536]{2,1,0:T(8,128)(2,1)S(1)}, bf16[1,8,1536]{2,1,0:T(8,128)(2,1)}, u32[]{:S(2)}) copy-start(bf16[1,8,1536]{2,1,0:T(8,128)(2,1)} %param.17) | copy-start | bytes 73732
  144.7 95.0 %copy-start.14 = (f32[1536]{0:T(1024)S(1)}, f32[1536]{0:T(1024)}, u32[]{:S(2)}) copy-start(f32[1536]{0:T(1024)} %param.30) | copy-start | bytes 18436
  144.7 62.8 %reduce-scatter.6.cloned.1.call-start = ((), (), s32[]{:S(2)}) async-start(), calls=%async_computation.4 | async-start | bytes 1769472 | tf_op jit(solution)/shard_map/reduce_scatter | solution.py:32
  160.8 121.1 %copy-start.27 = (s32[32]{0:T(128)S(1)}, s32[32]{0:T(128)}, u32[]{:S(2)}) copy-start(s32[32]{0:T(128)} %param.20) | copy-start | bytes 388
  160.8 123.1 %copy-start.17 = (s32[1,512]{1,0:T(1,128)S(1)}, s32[1,512]{1,0:T(1,128)}, u32[]{:S(2)}) copy-start(s32[1,512]{1,0:T(1,128)} %param.18) | copy-start | bytes 6148
  160.8 77.8 %reduce-scatter.8.cloned.1.call-start = ((), (), s32[]{:S(2)}) async-start(), calls=%async_computation.5 | async-start | bytes 245760 | tf_op jit(solution)/shard_map/reduce_scatter | solution.py:33
  207.5 90.1 %all-gather.9.cloned.1.call-start = ((), (), s32[]{:S(2)}) async-start(), calls=%async_computation.7 | async-start | bytes 2359296 | tf_op jit(solution)/shard_map/all_gather | solution.py:22
  239.6 62.1 %copy-start.4 = (bf16[1,8,1536]{2,1,0:T(8,128)(2,1)}, bf16[1,8,1536]{2,1,0:T(8,128)(2,1)S(1)}, u32[]{:S(2)}) copy-start(bf16[1,8,1536]{2,1,0:T(8,128)(2,1)S(1)} %get-tuple-element.254) | copy-start | bytes 73732
  301.7 62.3 %copy-start.7 = (s32[512]{0:T(512)S(1)}, s32[512]{0:T(512)}, u32[]{:S(2)}) copy-start(s32[512]{0:T(512)} %copy-done.6) | copy-start | bytes 6148
  (10 other events, 20.4 us)
Sparse Core Ops, SparseCore 0:
  55.9 16.4 all-gather.6
  144.8 15.9 reduce-scatter.3
  163.7 43.7 reduce-scatter.5
  210.1 28.4 reduce-scatter.7
  282.1 15.5 all-gather.8

commit v2 on v1

--- a/solution.py
+++ b/solution.py
@@ -37,8 +37,13 @@
     return lax.psum(lax.psum(lax.psum(values, "bc"), "by"), "bz")
 
 
-def max_blk(values):
-    return lax.pmax(lax.pmax(lax.pmax(values, "bc"), "by"), "bz")
+def combine_blk(top, expsum, target):
+    for axis in ("bc", "by", "bz"):
+        pieces = lax.all_gather(jnp.stack([top, expsum, target]), axis, axis=0)
+        top = jnp.max(pieces[:, 0], axis=0)
+        expsum = jnp.sum(pieces[:, 1] * jnp.exp(pieces[:, 0] - top[None]), axis=0)
+        target = jnp.sum(pieces[:, 2], axis=0)
+    return top, expsum, target
 
 
 def segments_of(lengths, count):
@@ -176,10 +181,15 @@
     final_carry, scanned = lax.scan(block_step, initial, scan_inputs)
     mixed = scanned.reshape(tokens_all, channels) + jnp.take(d_skip, channel_head) * conv_value
     gated = mixed * jax.nn.silu(gate_half)
-    squares = sum_blk(jnp.sum(gated * gated, axis=1))
-    inverse = lax.rsqrt(squares / inner_total + EPSILON)
-    gated_norm = (gated * inverse[:, None] * norm_gain).astype(jnp.bfloat16)
-    delta_own = scatter_rows(jnp.dot(gated_norm, w_out, preferred_element_type=jnp.float32))
+    squares = jnp.sum(gated * gated, axis=1)
+    gained = (gated * norm_gain).astype(jnp.bfloat16)
+    partial = jnp.dot(gained, w_out, preferred_element_type=jnp.float32)
+    packed = jnp.concatenate(
+        [partial, squares[:, None], jnp.zeros((tokens_all, 127), jnp.float32)], axis=1
+    )
+    packed_own = scatter_rows(packed)
+    inverse = lax.rsqrt(packed_own[:, D] / inner_total + EPSILON)
+    delta_own = packed_own[:, :D] * inverse[:, None]
     layer_own = (rows_own.astype(jnp.float32) + delta_own).astype(jnp.bfloat16)
     logits = jnp.dot(
         gather_rows(final_norm(layer_own, final_gain)),
@@ -191,9 +201,8 @@
     hit = jnp.arange(vocab_local, dtype=jnp.int32)[None, :] == local_label[:, None]
     target_local = jnp.sum(jnp.where(hit, logits, 0.0), axis=1)
     top_local = jnp.max(logits, axis=1)
-    top_all = max_blk(top_local)
-    expsum_local = jnp.sum(jnp.exp(logits - top_all[:, None]), axis=1)
-    expsum_all, target_all = sum_blk((expsum_local, target_local))
+    expsum_local = jnp.sum(jnp.exp(logits - top_local[:, None]), axis=1)
+    top_all, expsum_all, target_all = combine_blk(top_local, expsum_local, target_local)
     logprob = target_all - (top_all + jnp.log(expsum_all))
     token_own = lax.dynamic_slice_in_dim(logprob, blk_index * rows_count, rows_count, 0)
     seqs_count = lengths.shape[1]

time: 384 us -> 345 us (0.90)
  the two profiles are of different devices: /device:TPU:8 before, /device:TPU:16 now
where the time goes in v2:
time: 345 us; the launch traced here: 344 us
  blocking collectives  146 us (42%)
  waiting for transfers between devices  121 us (35%)
  local copies, waits for them, and re-layouts  25.2 us (7%)
  other arithmetic  20.3 us (6%)
  between operations  14.9 us (4%)
  matrix products  11.4 us (3%)
  loops' own time  5.35 us (2%)
    all_gather x2, blocking collectives, gather_rows(): part = lax.all_gather(part, 'by', axis=1)  58.3 us
    reduce_scatter x1, waiting for transfers between devices, scatter_rows(): part = lax.psum_scatter(part, 'by', scatter_dimension=1)  46.2 us
    all_gather x3, blocking collectives, combine_blk(): pieces = lax.all_gather(jnp.stack([top, expsum, target]), axis, axis=0)  43.6 us
    all_gather x2, blocking collectives, gather_rows(): part = lax.all_gather(rows, 'bz', axis=0)  33.3 us
    unnamed x6, waiting for transfers between devices  32.2 us
    reduce_scatter x1, waiting for transfers between devices, scatter_rows(): part = lax.psum_scatter(part, 'bc', scatter_dimension=2)  21.2 us
    all_gather x2, waiting for transfers between devices, gather_rows(): part = lax.all_gather(part, 'bc', axis=2)  21.1 us
    unnamed x1, blocking collectives  10.4 us
  transfers between devices with their start and end apart: 5, of which 5 were waited for; matrix products, arithmetic and copies ran while one was open for 3% of the time, Pallas kernels for 0%

profile of v2, /device:TPU:16, one launch (start us, length us, event | category | flops | bytes accessed | tf_op | source)
XLA Modules:
  0.0 343.7 jit_solution(3139894983571675741)
XLA Ops:
  7.3 19.6 %all_gather.51 = bf16[4,8,1536]{2,1,0:T(8,128)(2,1)S(1)} all-gather(bf16[1,8,1536]{2,1,0:T(8,128)(2,1)} %param.17), channel_id=1, replica_groups=mesh['bz'=4,'by'=8,'bc'=2,'seq'=4,'mp'=2] {'bz'}, dimensions={0}, use_global_device_ids=true | all-gather | bytes 122880 | tf_op jit(solution)/shard_map/all_gather | solution.py:20
  26.9 29.3 %all-gather = bf16[4,64,1536]{2,1,0:T(8,128)(2,1)} all-gather(bf16[4,8,1536]{2,1,0:T(8,128)(2,1)S(1)} %all_gather.51), channel_id=2, replica_groups=mesh['bz'=4,'by'=8,'bc'=2,'seq'=4,'mp'=2] {'by'}, dimensions={1}, use_global_device_ids=true | all-gather | bytes 884736 | tf_op jit(solution)/shard_map/all_gather | solution.py:21
  59.3 4.4 %compare_select_fusion.5 = s32[512,1]{0,1:T(1,128)S(1)} fusion(s32[]{:T(128)} %bitcast.15, s32[]{:T(128)} %bitcast.16, s32[]{:T(128)} %bitcast.17, s32[]{:T(128)} %bitcast.18, s32[]{:T(128)} %bitcast.19, s32[]{:T(128)} %bitcast.21, s32[]{:T(128)} %bitcast.20, s32[512,1]{0,1:T(1,128)S(1)} %bitcast.273, s32[512,1]{0,1:T(1,128)S(1)} %bitcast.268), kind=kLoop, calls=%fused_computation.144 | loop fusion | flops 7168 | bytes 6172 | tf_op jit(solution)/shard_map/jit(_take)/gather | solution.py:53
  64.3 7.9 %all-gather.14.cloned.1.call-done = bf16[4,8,16,1536]{3,2,1,0:T(8,128)(2,1)} async-done(((bf16[4,8,8,1536]{3,2,1,0:T(8,128)(2,1)}), bf16[4,8,16,1536]{3,2,1,0:T(8,128)(2,1)}) %all-gather.14.cloned.1.call-update) | async-done | bytes 1572880 | tf_op jit(solution)/shard_map/all_gather | solution.py:22
  72.3 2.5 convolution_convert_fusion
  79.1 29.3 %while.17 = (s32[]{:T(128)}, f32[48,128]{1,0:T(8,128)S(1)}, s32[]{:T(128)}, f32[2,256,48]{1,0,2:T(2,128)}, s32[2,256]{1,0:T(2,128)}, /*index=5*/f32[2,256,2]{1,2...) while((s32[]{:T(128)}, f32[48,128]{1,0:T(8,128)S(1)}, ...), condition=%wide.region_5.6_spmd.clone.clone.clone, body=%wide.region_2.5_spmd.clone.clone.clone.sunk | while | flops 215140816 | bytes 2177448 | solution.py:181
  86.2 1.9 compare_convert_fusion.10
  89.1 2.2 dynamic_update_slice.8
  100.8 1.9 compare_convert_fusion.10
  103.7 2.2 dynamic_update_slice.8
  110.1 1.3 fusion.75
  111.5 1.9 copy.52
  113.9 4.3 %concatenate.38 = f32[4,8,2,8,1664]{4,3,0,1,2:T(8,128)} concatenate(f32[4,8,2,8,1536]{4,3,0,1,2:T(8,128)} %copy.52, f32[4,8,2,8,1]{4,3,0,1,2:T(8,128)S(1)} %copy.53, f32[4,8,2,8,127]{4,3,0,1,2:T(8,128)S(1)} %broadcast_in_dim.33), dimensions={4} | concatenate | bytes 6815744 | tf_op jit(solution)/shard_map/concatenate | solution.py:187
  118.3 21.2 %reduce-scatter.6.cloned.1.call-done = f32[4,8,1,8,1664]{4,3,0,1,2:T(8,128)} async-done(((f32[4,8,2,8,1664]{4,3,0,1,2:T(8,128)}), f32[4,8,1,8,1664]{4,3,0,1,2:T(8,128)}) %reduce-scatter.6.cloned.1.call-update) | async-done | bytes 1703952 | tf_op jit(solution)/shard_map/reduce_scatter | solution.py:31
  139.6 46.2 %reduce-scatter.8.cloned.1.call-done = f32[4,1,8,1664]{3,2,0,1:T(8,128)} async-done(((f32[4,8,8,1664]{3,2,0,1:T(8,128)}), f32[4,1,8,1664]{3,2,0,1:T(8,128)}) %reduce-scatter.8.cloned.1.call-update) | async-done | bytes 213008 | tf_op jit(solution)/shard_map/reduce_scatter | solution.py:32
  185.8 32.1 %reduce-scatter.10.cloned.1.call-done = f32[1,8,1664]{2,1,0:T(8,128)} async-done(((f32[4,8,1664]{2,1,0:T(8,128)}), f32[1,8,1664]{2,1,0:T(8,128)}) %reduce-scatter.10.cloned.1.call-update) | async-done | bytes 53264
  219.8 13.7 %all-gather.2 = bf16[32,1536]{1,0:T(8,128)(2,1)S(1)} all-gather(bf16[8,1536]{1,0:T(8,128)(2,1)S(1)} %fusion.74), channel_id=4, replica_groups=mesh['bz'=4,'by'=8,'bc'=2,'seq'=4,'mp'=2] {'bz'}, dimensions={0}, use_global_device_ids=true | all-gather | bytes 122880 | tf_op jit(solution)/shard_map/all_gather | solution.py:20
  233.5 29.1 %all-gather.3 = bf16[4,64,1536]{2,1,0:T(8,128)(2,1)} all-gather(bf16[4,8,1536]{2,1,0:T(8,128)(2,1)S(1)} %bitcast.247), channel_id=5, replica_groups=mesh['bz'=4,'by'=8,'bc'=2,'seq'=4,'mp'=2] {'by'}, dimensions={1}, use_global_device_ids=true | all-gather | bytes 884736 | tf_op jit(solution)/shard_map/all_gather | solution.py:21
  264.7 13.2 %all-gather.16.cloned.1.call-done = bf16[4,8,16,1536]{3,2,1,0:T(8,128)(2,1)} async-done(((bf16[4,8,8,1536]{3,2,1,0:T(8,128)(2,1)}), bf16[4,8,16,1536]{3,2,1,0:T(8,128)(2,1)}) %all-gather.16.cloned.1.call-update) | async-done | bytes 1572880 | tf_op jit(solution)/shard_map/all_gather | solution.py:22
  277.9 2.9 fusion.107
  281.3 1.8 all-gather.8
  283.2 25.5 %all-gather.9 = f32[8,3,512]{2,1,0:T(4,128)S(1)} all-gather(f32[1,3,512]{2,1,0:T(4,128)S(1)} %maximum_bitcast_fusion.1), channel_id=8, replica_groups=mesh['bz'=4,'by'=8,'bc'=2,'seq'=4,'mp'=2] {'by'}, dimensions={0}, use_global_device_ids=true | all-gather | bytes 55296 | tf_op jit(solution)/shard_map/all_gather | solution.py:42
  308.8 16.2 %all-gather.10 = f32[4,3,512]{2,1,0:T(4,128)S(1)} all-gather(f32[1,3,512]{2,1,0:T(4,128)S(1)} %maximum_bitcast_fusion.2), channel_id=9, replica_groups=mesh['bz'=4,'by'=8,'bc'=2,'seq'=4,'mp'=2] {'bz'}, dimensions={0}, use_global_device_ids=true | all-gather | bytes 30720 | tf_op jit(solution)/shard_map/all_gather | solution.py:42
  325.6 10.4 %all-reduce.7 = f32[32]{0:T(128)S(1)} all-reduce(f32[32]{0:T(128)S(1)} %convolution_bitcast_fusion.1), channel_id=13, replica_groups=mesh['bz'=4,'by'=8,'bc'=2,'seq'=4,'mp'=2] {'seq'}, use_global_device_ids=true, to_apply=%region_23.24.clone | all-reduce | flops 32 | bytes 256
  (153 shorter events, 31.6 us)
Async XLA Ops:
  7.2 270.7 %copy-start = (bf16[1536,786]{0,1:T(8,128)(2,1)S(1)}, bf16[1536,786]{0,1:T(8,128)(2,1)}, u32[]{:S(2)}) copy-start(bf16[1536,786]{0,1:T(8,128)(2,1)} %param.31) | copy-start | bytes 7243780
  7.2 49.1 %copy-start.19 = (s32[1,8]{1,0:T(1,128)S(1)}, s32[1,8]{1,0:T(1,128)}, u32[]{:S(2)}) copy-start(s32[1,8]{1,0:T(1,128)} %param.19) | copy-start | bytes 100
  7.2 50.0 %copy-start.1 = (f32[48]{0:T(128)S(1)}, f32[48]{0:T(128)}, u32[]{:S(2)}) copy-start(f32[48]{0:T(128)} %param.27) | copy-start | bytes 580
  7.2 52.1 %copy-start.15 = (f32[4,48]{1,0:T(4,128)S(1)}, f32[4,48]{1,0:T(4,128)}, u32[]{:S(2)}) copy-start(f32[4,48]{1,0:T(4,128)} %param.23) | copy-start | bytes 2308
  7.2 57.1 %copy-start.14 = (f32[4,256]{1,0:T(4,128)S(1)}, f32[4,256]{1,0:T(4,128)}, u32[]{:S(2)}) copy-start(f32[4,256]{1,0:T(4,128)} %param.24) | copy-start | bytes 12292
  7.2 65.1 %all-gather.14.cloned.1.call-start = ((), (), s32[]{:S(2)}) async-start(), calls=%async_computation.5 | async-start | bytes 2359296 | tf_op jit(solution)/shard_map/all_gather | solution.py:22
  56.2 83.3 %reduce-scatter.6.cloned.1.call-start = ((), (), s32[]{:S(2)}) async-start(), calls=%async_computation.3 | async-start | bytes 5111808 | tf_op jit(solution)/shard_map/reduce_scatter | solution.py:31
  56.5 18.2 %copy-start.11 = (s32[512]{0:T(512)}, s32[512]{0:T(512)S(1)}, u32[]{:S(2)}) copy-start(s32[512]{0:T(512)S(1)} %get-tuple-element.304) | copy-start | bytes 6148
  72.3 2.5 copy-start.2
  72.3 2.5 copy-start.6
  75.4 2.8 copy-start.3
  79.1 30.2 %copy-start.4 = (bf16[512,96]{0,1:T(8,128)(2,1)S(1)}, bf16[512,96]{0,1:T(8,128)(2,1)}, u32[]{:S(2)}) copy-start(bf16[512,96]{0,1:T(8,128)(2,1)} %copy-done.3) | copy-start | bytes 294916
  79.1 30.2 %copy-start.5 = (f32[512,48]{0,1:T(8,128)S(1)}, f32[512,48]{0,1:T(8,128)}, u32[]{:S(2)}) copy-start(f32[512,48]{0,1:T(8,128)} %get-tuple-element.258) | copy-start | bytes 294916
  79.1 31.0 %copy-start.7 = (bf16[48,1536]{1,0:T(8,128)(2,1)S(1)}, bf16[48,1536]{1,0:T(8,128)(2,1)}, u32[]{:S(2)}) copy-start(bf16[48,1536]{1,0:T(8,128)(2,1)} %param.29) | copy-start | bytes 442372
  83.9 1.0 copy-start.8
  118.3 100.4 %copy-start.10 = (bf16[1,8,1536]{2,1,0:T(8,128)(2,1)S(1)}, bf16[1,8,1536]{2,1,0:T(8,128)(2,1)}, u32[]{:S(2)}) copy-start(bf16[1,8,1536]{2,1,0:T(8,128)(2,1)} %param.17) | copy-start | bytes 73732
  118.3 101.4 %copy-start.13 = (f32[1536]{0:T(1024)S(1)}, f32[1536]{0:T(1024)}, u32[]{:S(2)}) copy-start(f32[1536]{0:T(1024)} %param.30) | copy-start | bytes 18436
  118.3 67.5 %reduce-scatter.8.cloned.1.call-start = ((), (), s32[]{:S(2)}) async-start(), calls=%async_computation.4 | async-start | bytes 1916928 | tf_op jit(solution)/shard_map/reduce_scatter | solution.py:32
  139.5 123.2 %copy-start.20 = (s32[32]{0:T(128)S(1)}, s32[32]{0:T(128)}, u32[]{:S(2)}) copy-start(s32[32]{0:T(128)} %param.20) | copy-start | bytes 388
  139.5 125.2 %copy-start.16 = (s32[1,512]{1,0:T(1,128)S(1)}, s32[1,512]{1,0:T(1,128)}, u32[]{:S(2)}) copy-start(s32[1,512]{1,0:T(1,128)} %param.18) | copy-start | bytes 6148
  139.5 78.4 %reduce-scatter.10.cloned.1.call-start = ((), (), s32[]{:S(2)}) async-start(), calls=%async_computation.7 | async-start | bytes 266240
  185.8 92.1 %all-gather.16.cloned.1.call-start = ((), (), s32[]{:S(2)}) async-start(), calls=%async_computation.6 | async-start | bytes 2359296 | tf_op jit(solution)/shard_map/all_gather | solution.py:22
  219.7 61.1 %copy-start.9 = (bf16[8,1536]{1,0:T(8,128)(2,1)}, bf16[8,1536]{1,0:T(8,128)(2,1)S(1)}, u32[]{:S(2)}) copy-start(bf16[8,1536]{1,0:T(8,128)(2,1)S(1)} %get-tuple-element.254) | copy-start | bytes 73732
  280.8 44.4 %copy-start.12 = (s32[512]{0:T(512)S(1)}, s32[512]{0:T(512)}, u32[]{:S(2)}) copy-start(s32[512]{0:T(512)} %copy-done.11) | copy-start | bytes 6148
  (3 other events, 2.5 us)
Sparse Core Ops, SparseCore 0:
  56.3 15.9 all-gather.13
  118.4 21.0 reduce-scatter.5
  142.4 43.3 reduce-scatter.7
  188.4 29.4 reduce-scatter.9
  262.8 15.0 all-gather.15

commit v3 on v2

--- a/solution.py
+++ b/solution.py
@@ -7,7 +7,7 @@
 D = 1536
 HEADDIM = 64
 NSTATE = 128
-SCAN_BLOCK = 256
+SCAN_BLOCK = 512
 CONV = 4
 
 

time: 345 us -> 318 us (0.922)
  local copies, waits for them, and re-layouts: 25.2 us -> 11.6 us
  other arithmetic: 20.3 us -> 10.3 us
  loops' own time: 5.35 us -> 0 us
    another operation x1 -> x0, loops' own time: 5.35 us -> none  [shards(): final_carry, scanned = lax.scan(block_step, initial, scan_inputs)]
    dynamic_update_slice x4 -> x0, local copies, waits for them, and re-layouts: 4.53 us -> none  [shards(): final_carry, scanned = lax.scan(block_step, initial, scan_inputs)]
    convert_element_type x2 -> x0, other arithmetic: 3.9 us -> none  [block_step(): leading = (seg_block == seg_block[0]).astype(jnp.float32)[:, None]]
where the time goes in v3:
time: 318 us; the launch traced here: 317 us
  blocking collectives  146 us (46%)
  waiting for transfers between devices  121 us (38%)
  between operations  14.9 us (5%)
  matrix products  13.6 us (4%)
  local copies, waits for them, and re-layouts  11.6 us (4%)
  other arithmetic  10.3 us (3%)
    all_gather x2, blocking collectives, gather_rows(): part = lax.all_gather(part, 'by', axis=1)  58.4 us
    reduce_scatter x1, waiting for transfers between devices, scatter_rows(): part = lax.psum_scatter(part, 'by', scatter_dimension=1)  46.1 us
    all_gather x3, blocking collectives, combine_blk(): pieces = lax.all_gather(jnp.stack([top, expsum, target]), axis, axis=0)  43.6 us
    all_gather x2, blocking collectives, gather_rows(): part = lax.all_gather(rows, 'bz', axis=0)  33.3 us
    unnamed x6, waiting for transfers between devices  32.3 us
    all_gather x2, waiting for transfers between devices, gather_rows(): part = lax.all_gather(part, 'bc', axis=2)  21.2 us
    reduce_scatter x1, waiting for transfers between devices, scatter_rows(): part = lax.psum_scatter(part, 'bc', scatter_dimension=2)  21.2 us
    unnamed x1, blocking collectives  10.4 us
  transfers between devices with their start and end apart: 5, of which 5 were waited for; matrix products, arithmetic and copies ran while one was open for 3% of the time, Pallas kernels for 0%

profile of v3, /device:TPU:16, one launch (start us, length us, event | category | flops | bytes accessed | tf_op | source)
XLA Modules:
  0.0 317.0 jit_solution(6762370134211868574)
XLA Ops:
  7.3 19.6 %all_gather.51 = bf16[4,8,1536]{2,1,0:T(8,128)(2,1)S(1)} all-gather(bf16[1,8,1536]{2,1,0:T(8,128)(2,1)} %param.15), channel_id=1, replica_groups=mesh['bz'=4,'by'=8,'bc'=2,'seq'=4,'mp'=2] {'bz'}, dimensions={0}, use_global_device_ids=true | all-gather | bytes 122880 | tf_op jit(solution)/shard_map/all_gather | solution.py:20
  26.9 29.3 %all-gather = bf16[4,64,1536]{2,1,0:T(8,128)(2,1)} all-gather(bf16[4,8,1536]{2,1,0:T(8,128)(2,1)S(1)} %all_gather.51), channel_id=2, replica_groups=mesh['bz'=4,'by'=8,'bc'=2,'seq'=4,'mp'=2] {'by'}, dimensions={1}, use_global_device_ids=true | all-gather | bytes 884736 | tf_op jit(solution)/shard_map/all_gather | solution.py:21
  58.6 4.4 %compare_select_fusion.2 = s32[512,1]{0,1:T(1,128)S(1)} fusion(s32[]{:T(128)} %bitcast.13, s32[]{:T(128)} %bitcast.14, s32[]{:T(128)} %bitcast.15, s32[]{:T(128)} %bitcast.16, s32[]{:T(128)} %bitcast.17, s32[]{:T(128)} %bitcast.19, s32[]{:T(128)} %bitcast.18, s32[512,1]{0,1:T(1,128)S(1)} %bitcast.173, s32[512,1]{0,1:T(1,128)S(1)} %bitcast.171), kind=kLoop, calls=%fused_computation.96 | loop fusion | flops 7168 | bytes 6172 | tf_op jit(solution)/shard_map/jit(_take)/gather | solution.py:53
  63.0 1.2 compare_convert_fusion.4
  64.3 8.0 %all-gather.14.cloned.1.call-done = bf16[4,8,16,1536]{3,2,1,0:T(8,128)(2,1)} async-done(((bf16[4,8,8,1536]{3,2,1,0:T(8,128)(2,1)}), bf16[4,8,16,1536]{3,2,1,0:T(8,128)(2,1)}) %all-gather.14.cloned.1.call-update) | async-done | bytes 1572880 | tf_op jit(solution)/shard_map/all_gather | solution.py:22
  72.3 2.3 convolution_convert_fusion
  75.4 2.0 fusion.27
  78.7 2.1 convolution_convert_fusion.1
  81.1 1.5 fusion.8
  82.6 1.5 multiply_reduce_fusion
  84.7 1.9 copy.32
  87.2 4.3 %concatenate.38 = f32[4,8,2,8,1664]{4,3,0,1,2:T(8,128)} concatenate(f32[4,8,2,8,1536]{4,3,0,1,2:T(8,128)} %copy.32, f32[4,8,2,8,1]{4,3,0,1,2:T(8,128)S(1)} %copy.33, f32[4,8,2,8,127]{4,3,0,1,2:T(8,128)S(1)} %broadcast_in_dim.34), dimensions={4} | concatenate | bytes 6815744 | tf_op jit(solution)/shard_map/concatenate | solution.py:187
  91.6 21.2 %reduce-scatter.6.cloned.1.call-done = f32[4,8,1,8,1664]{4,3,0,1,2:T(8,128)} async-done(((f32[4,8,2,8,1664]{4,3,0,1,2:T(8,128)}), f32[4,8,1,8,1664]{4,3,0,1,2:T(8,128)}) %reduce-scatter.6.cloned.1.call-update) | async-done | bytes 1703952 | tf_op jit(solution)/shard_map/reduce_scatter | solution.py:31
  112.9 46.1 %reduce-scatter.8.cloned.1.call-done = f32[4,1,8,1664]{3,2,0,1:T(8,128)} async-done(((f32[4,8,8,1664]{3,2,0,1:T(8,128)}), f32[4,1,8,1664]{3,2,0,1:T(8,128)}) %reduce-scatter.8.cloned.1.call-update) | async-done | bytes 213008 | tf_op jit(solution)/shard_map/reduce_scatter | solution.py:32
  159.0 32.2 %reduce-scatter.10.cloned.1.call-done = f32[1,8,1664]{2,1,0:T(8,128)} async-done(((f32[4,8,1664]{2,1,0:T(8,128)}), f32[1,8,1664]{2,1,0:T(8,128)}) %reduce-scatter.10.cloned.1.call-update) | async-done | bytes 53264
  193.1 13.7 %all-gather.2 = bf16[32,1536]{1,0:T(8,128)(2,1)S(1)} all-gather(bf16[8,1536]{1,0:T(8,128)(2,1)S(1)} %fusion.39), channel_id=4, replica_groups=mesh['bz'=4,'by'=8,'bc'=2,'seq'=4,'mp'=2] {'bz'}, dimensions={0}, use_global_device_ids=true | all-gather | bytes 122880 | tf_op jit(solution)/shard_map/all_gather | solution.py:20
  206.8 29.1 %all-gather.3 = bf16[4,64,1536]{2,1,0:T(8,128)(2,1)} all-gather(bf16[4,8,1536]{2,1,0:T(8,128)(2,1)S(1)} %bitcast.157), channel_id=5, replica_groups=mesh['bz'=4,'by'=8,'bc'=2,'seq'=4,'mp'=2] {'by'}, dimensions={1}, use_global_device_ids=true | all-gather | bytes 884736 | tf_op jit(solution)/shard_map/all_gather | solution.py:21
  236.0 1.3 dynamic-slice.7
  238.0 13.2 %all-gather.16.cloned.1.call-done = bf16[4,8,16,1536]{3,2,1,0:T(8,128)(2,1)} async-done(((bf16[4,8,8,1536]{3,2,1,0:T(8,128)(2,1)}), bf16[4,8,16,1536]{3,2,1,0:T(8,128)(2,1)}) %all-gather.16.cloned.1.call-update) | async-done | bytes 1572880 | tf_op jit(solution)/shard_map/all_gather | solution.py:22
  251.2 2.9 fusion.81
  254.5 1.8 all-gather.8
  256.4 25.5 %all-gather.9 = f32[8,3,512]{2,1,0:T(4,128)S(1)} all-gather(f32[1,3,512]{2,1,0:T(4,128)S(1)} %maximum_bitcast_fusion.1), channel_id=8, replica_groups=mesh['bz'=4,'by'=8,'bc'=2,'seq'=4,'mp'=2] {'by'}, dimensions={0}, use_global_device_ids=true | all-gather | bytes 55296 | tf_op jit(solution)/shard_map/all_gather | solution.py:42
  282.1 16.3 %all-gather.10 = f32[4,3,512]{2,1,0:T(4,128)S(1)} all-gather(f32[1,3,512]{2,1,0:T(4,128)S(1)} %maximum_bitcast_fusion.2), channel_id=9, replica_groups=mesh['bz'=4,'by'=8,'bc'=2,'seq'=4,'mp'=2] {'bz'}, dimensions={0}, use_global_device_ids=true | all-gather | bytes 30720 | tf_op jit(solution)/shard_map/all_gather | solution.py:42
  298.9 10.4 %all-reduce.7 = f32[32]{0:T(128)S(1)} all-reduce(f32[32]{0:T(128)S(1)} %convolution_bitcast_fusion.1), channel_id=13, replica_groups=mesh['bz'=4,'by'=8,'bc'=2,'seq'=4,'mp'=2] {'seq'}, use_global_device_ids=true, to_apply=%region_21.22.clone | all-reduce | flops 32 | bytes 256
  (96 shorter events, 10.4 us)
Async XLA Ops:
  7.2 244.0 %copy-start = (bf16[1536,786]{0,1:T(8,128)(2,1)S(1)}, bf16[1536,786]{0,1:T(8,128)(2,1)}, u32[]{:S(2)}) copy-start(bf16[1536,786]{0,1:T(8,128)(2,1)} %param.29) | copy-start | bytes 7243780
  7.2 49.0 %copy-start.14 = (s32[1,8]{1,0:T(1,128)S(1)}, s32[1,8]{1,0:T(1,128)}, u32[]{:S(2)}) copy-start(s32[1,8]{1,0:T(1,128)} %param.17) | copy-start | bytes 100
  7.2 49.9 %copy-start.1 = (f32[48]{0:T(128)S(1)}, f32[48]{0:T(128)}, u32[]{:S(2)}) copy-start(f32[48]{0:T(128)} %param.25) | copy-start | bytes 580
  7.2 51.4 %copy-start.9 = (f32[4,48]{1,0:T(4,128)S(1)}, f32[4,48]{1,0:T(4,128)}, u32[]{:S(2)}) copy-start(f32[4,48]{1,0:T(4,128)} %param.21) | copy-start | bytes 2308
  7.2 57.0 %copy-start.8 = (f32[4,256]{1,0:T(4,128)S(1)}, f32[4,256]{1,0:T(4,128)}, u32[]{:S(2)}) copy-start(f32[4,256]{1,0:T(4,128)} %param.22) | copy-start | bytes 12292
  7.2 65.1 %all-gather.14.cloned.1.call-start = ((), (), s32[]{:S(2)}) async-start(), calls=%async_computation.5 | async-start | bytes 2359296 | tf_op jit(solution)/shard_map/all_gather | solution.py:22
  56.2 56.6 %reduce-scatter.6.cloned.1.call-start = ((), (), s32[]{:S(2)}) async-start(), calls=%async_computation.3 | async-start | bytes 5111808 | tf_op jit(solution)/shard_map/reduce_scatter | solution.py:31
  74.7 2.7 copy-start.11
  74.7 2.7 copy-start.12
  74.7 4.0 %copy-start.3 = (bf16[1536,2,48]{0,2,1:T(8,128)(2,1)S(1)}, bf16[1536,2,48]{0,2,1:T(8,128)(2,1)}, u32[]{:S(2)}) copy-start(bf16[1536,2,48]{0,2,1:T(8,128)(2,1)} %param.19) | copy-start | bytes 884740
  78.6 2.5 copy-start.2
  82.5 1.5 copy-start.4
  82.6 1.5 copy-start.13
  91.6 100.4 %copy-start.6 = (bf16[1,8,1536]{2,1,0:T(8,128)(2,1)S(1)}, bf16[1,8,1536]{2,1,0:T(8,128)(2,1)}, u32[]{:S(2)}) copy-start(bf16[1,8,1536]{2,1,0:T(8,128)(2,1)} %param.15) | copy-start | bytes 73732
  91.6 101.4 %copy-start.7 = (f32[1536]{0:T(1024)S(1)}, f32[1536]{0:T(1024)}, u32[]{:S(2)}) copy-start(f32[1536]{0:T(1024)} %param.28) | copy-start | bytes 18436
  91.6 67.3 %reduce-scatter.8.cloned.1.call-start = ((), (), s32[]{:S(2)}) async-start(), calls=%async_computation.4 | async-start | bytes 1916928 | tf_op jit(solution)/shard_map/reduce_scatter | solution.py:32
  112.8 123.1 %copy-start.15 = (s32[32]{0:T(128)S(1)}, s32[32]{0:T(128)}, u32[]{:S(2)}) copy-start(s32[32]{0:T(128)} %param.18) | copy-start | bytes 388
  112.8 125.1 %copy-start.10 = (s32[1,512]{1,0:T(1,128)S(1)}, s32[1,512]{1,0:T(1,128)}, u32[]{:S(2)}) copy-start(s32[1,512]{1,0:T(1,128)} %param.16) | copy-start | bytes 6148
  112.8 78.4 %reduce-scatter.10.cloned.1.call-start = ((), (), s32[]{:S(2)}) async-start(), calls=%async_computation.7 | async-start | bytes 266240
  158.9 92.2 %all-gather.16.cloned.1.call-start = ((), (), s32[]{:S(2)}) async-start(), calls=%async_computation.6 | async-start | bytes 2359296 | tf_op jit(solution)/shard_map/all_gather | solution.py:22
  193.0 61.1 %copy-start.5 = (bf16[8,1536]{1,0:T(8,128)(2,1)}, bf16[8,1536]{1,0:T(8,128)(2,1)S(1)}, u32[]{:S(2)}) copy-start(bf16[8,1536]{1,0:T(8,128)(2,1)S(1)} %get-tuple-element.48) | copy-start | bytes 73732
Sparse Core Ops, SparseCore 0:
  56.3 15.9 all-gather.13
  91.7 21.0 reduce-scatter.5
  115.6 43.2 reduce-scatter.7
  161.6 29.5 reduce-scatter.9
  236.0 15.0 all-gather.15

commit v4 on v3

--- a/solution.py
+++ b/solution.py
@@ -183,11 +183,27 @@
     gated = mixed * jax.nn.silu(gate_half)
     squares = jnp.sum(gated * gated, axis=1)
     gained = (gated * norm_gain).astype(jnp.bfloat16)
-    partial = jnp.dot(gained, w_out, preferred_element_type=jnp.float32)
+    square_high = squares.astype(jnp.bfloat16)
+    square_low = (squares - square_high.astype(jnp.float32)).astype(jnp.bfloat16)
+    sent = jnp.concatenate([gained, square_high[:, None], square_low[:, None]], axis=1)
+    bz = lax.axis_size("bz")
+    by = lax.axis_size("by")
+    bc = lax.axis_size("bc")
+    sent = sent.reshape(bz, by, bc, rows_count, channels + 2)
+    both = lax.all_gather(sent, "bc", axis=0)
+    mine = lax.dynamic_index_in_dim(both, lax.axis_index("bc"), axis=3, keepdims=False)
+    mine = jnp.transpose(mine, (2, 1, 3, 0, 4))
+    half_rows = bz * by * rows_count
+    gained_pair = mine[..., :channels].reshape(half_rows, bc * channels)
+    squares_pair = jnp.sum(mine[..., channels:].astype(jnp.float32), axis=(3, 4)).reshape(half_rows)
+    w_pair = lax.all_gather(w_out, "bc", axis=0, tiled=True)
+    partial = jnp.dot(gained_pair, w_pair, preferred_element_type=jnp.float32)
     packed = jnp.concatenate(
-        [partial, squares[:, None], jnp.zeros((tokens_all, 127), jnp.float32)], axis=1
-    )
-    packed_own = scatter_rows(packed)
+        [partial, squares_pair[:, None], jnp.zeros((half_rows, 127), jnp.float32)], axis=1
+    )
+    packed = packed.reshape(by, bz, rows_count, D + 128)
+    packed = lax.psum_scatter(packed, "by", scatter_dimension=0)
+    packed_own = lax.psum_scatter(packed, "bz", scatter_dimension=0)
     inverse = lax.rsqrt(packed_own[:, D] / inner_total + EPSILON)
     delta_own = packed_own[:, :D] * inverse[:, None]
     layer_own = (rows_own.astype(jnp.float32) + delta_own).astype(jnp.bfloat16)

time: 318 us -> 294 us (0.925)
  waiting for transfers between devices: 121 us -> 94.9 us
  blocking collectives: 146 us -> 150 us
    reduce_scatter x2 -> x1, waiting for transfers between devices: 67.2 us -> 43.5 us  [shards(): packed = lax.psum_scatter(packed, 'by', scatter_dimension=0)]
    concatenate x4 -> x2, local copies, waits for them, and re-layouts: 6.75 us -> 2.68 us  [shards(): jnp.concatenate([partial, squares_pair[:, None], jnp.zeros((half_rows, 12...]
    all_gather x0 -> x2, blocking collectives: none -> 4.01 us  [the longest x1 2.02 us: shards(): w_pair = lax.all_gather(w_out, 'bc', axis=0, tiled=True)]
    unnamed x6 -> x5, waiting for transfers between devices: 32.3 us -> 32.2 us
  transfers between devices with their start and end apart: 5 -> 4, of which waited for: 5 -> 4; matrix products, arithmetic and copies ran while one was open for 3% -> 3% of each run, Pallas kernels for 0% -> 0%
where the time goes in v4:
time: 294 us
  blocking collectives  150 us (51%)
  waiting for transfers between devices  94.9 us (32%)
  between operations  14.9 us (5%)
  matrix products  13.1 us (4%)
  other arithmetic  11.6 us (4%)
  local copies, waits for them, and re-layouts  9.54 us (3%)
    all_gather x2, blocking collectives, gather_rows(): part = lax.all_gather(part, 'by', axis=1)  58.4 us
    all_gather x3, blocking collectives, combine_blk(): pieces = lax.all_gather(jnp.stack([top, expsum, target]), axis, axis=0)  43.6 us
    reduce_scatter x1, waiting for transfers between devices, shards(): packed = lax.psum_scatter(packed, 'by', scatter_dimension=0)  43.5 us
    all_gather x2, blocking collectives, gather_rows(): part = lax.all_gather(rows, 'bz', axis=0)  33.3 us
    unnamed x5, waiting for transfers between devices  32.2 us
    all_gather x2, waiting for transfers between devices, gather_rows(): part = lax.all_gather(part, 'bc', axis=2)  19.1 us
    unnamed x1, blocking collectives  10.4 us
  transfers between devices with their start and end apart: 4, of which 4 were waited for; matrix products, arithmetic and copies ran while one was open for 3% of the time, Pallas kernels for 0%

profile of v4, /device:TPU:16, one launch (start us, length us, event | category | flops | bytes accessed | tf_op | source)
XLA Modules:
  0.0 293.9 jit_solution(5805046161435891865)
XLA Ops:
  7.3 19.6 %all_gather.57 = bf16[4,8,1536]{2,1,0:T(8,128)(2,1)S(1)} all-gather(bf16[1,8,1536]{2,1,0:T(8,128)(2,1)} %param.15), channel_id=1, replica_groups=mesh['bz'=4,'by'=8,'bc'=2,'seq'=4,'mp'=2] {'bz'}, dimensions={0}, use_global_device_ids=true | all-gather | bytes 122880 | tf_op jit(solution)/shard_map/all_gather | solution.py:20
  26.9 29.3 %all-gather = bf16[4,64,1536]{2,1,0:T(8,128)(2,1)} all-gather(bf16[4,8,1536]{2,1,0:T(8,128)(2,1)S(1)} %all_gather.57), channel_id=2, replica_groups=mesh['bz'=4,'by'=8,'bc'=2,'seq'=4,'mp'=2] {'by'}, dimensions={1}, use_global_device_ids=true | all-gather | bytes 884736 | tf_op jit(solution)/shard_map/all_gather | solution.py:21
  56.6 2.0 all_gather.63
  60.6 4.4 %compare_select_fusion.2 = s32[512,1]{0,1:T(1,128)S(1)} fusion(s32[]{:T(128)} %bitcast.13, s32[]{:T(128)} %bitcast.14, s32[]{:T(128)} %bitcast.15, s32[]{:T(128)} %bitcast.16, s32[]{:T(128)} %bitcast.17, s32[]{:T(128)} %bitcast.19, s32[]{:T(128)} %bitcast.18, s32[512,1]{0,1:T(1,128)S(1)} %bitcast.186, s32[512,1]{0,1:T(1,128)S(1)} %bitcast.184), kind=kLoop, calls=%fused_computation.101 | loop fusion | flops 7168 | bytes 6172 | tf_op jit(solution)/shard_map/jit(_take)/gather | solution.py:53
  66.3 6.0 %all-gather.14.cloned.1.call-done = bf16[4,8,16,1536]{3,2,1,0:T(8,128)(2,1)} async-done(((bf16[4,8,8,1536]{3,2,1,0:T(8,128)(2,1)}), bf16[4,8,16,1536]{3,2,1,0:T(8,128)(2,1)}) %all-gather.14.cloned.1.call-update) | async-done | bytes 1572880 | tf_op jit(solution)/shard_map/all_gather | solution.py:22
  72.3 2.1 convolution_convert_fusion.1
  74.5 1.9 convolution_convert_fusion
  78.3 1.6 divide_multiply_fusion
  81.3 1.5 fusion.8
  82.8 1.5 multiply_convert_fusion
  85.6 2.0 all_gather.62
  88.4 1.5 fusion.27
  89.9 2.4 concatenate.43
  92.4 43.5 %reduce-scatter.5.cloned.1.call-done = f32[1,4,8,1664]{3,2,1,0:T(8,128)} async-done(((f32[8,4,8,1664]{3,2,1,0:T(8,128)}), f32[1,4,8,1664]{3,2,1,0:T(8,128)}) %reduce-scatter.5.cloned.1.call-update) | async-done | bytes 213008 | tf_op jit(solution)/shard_map/reduce_scatter | solution.py:205
  136.0 32.1 %reduce-scatter.7.cloned.1.call-done = f32[1,8,1664]{2,1,0:T(8,128)} async-done(((f32[4,8,1664]{2,1,0:T(8,128)}), f32[1,8,1664]{2,1,0:T(8,128)}) %reduce-scatter.7.cloned.1.call-update) | async-done | bytes 53264
  170.1 13.7 %all-gather.2 = bf16[32,1536]{1,0:T(8,128)(2,1)S(1)} all-gather(bf16[8,1536]{1,0:T(8,128)(2,1)S(1)} %fusion.41), channel_id=4, replica_groups=mesh['bz'=4,'by'=8,'bc'=2,'seq'=4,'mp'=2] {'bz'}, dimensions={0}, use_global_device_ids=true | all-gather | bytes 122880 | tf_op jit(solution)/shard_map/all_gather | solution.py:20
  183.8 29.1 %all-gather.3 = bf16[4,64,1536]{2,1,0:T(8,128)(2,1)} all-gather(bf16[4,8,1536]{2,1,0:T(8,128)(2,1)S(1)} %bitcast.169), channel_id=5, replica_groups=mesh['bz'=4,'by'=8,'bc'=2,'seq'=4,'mp'=2] {'by'}, dimensions={1}, use_global_device_ids=true | all-gather | bytes 884736 | tf_op jit(solution)/shard_map/all_gather | solution.py:21
  213.0 1.3 dynamic-slice.7
  215.0 13.1 %all-gather.16.cloned.1.call-done = bf16[4,8,16,1536]{3,2,1,0:T(8,128)(2,1)} async-done(((bf16[4,8,8,1536]{3,2,1,0:T(8,128)(2,1)}), bf16[4,8,16,1536]{3,2,1,0:T(8,128)(2,1)}) %all-gather.16.cloned.1.call-update) | async-done | bytes 1572880 | tf_op jit(solution)/shard_map/all_gather | solution.py:22
  228.1 2.9 fusion.81
  231.4 1.8 all-gather.8
  233.3 25.5 %all-gather.9 = f32[8,3,512]{2,1,0:T(4,128)S(1)} all-gather(f32[1,3,512]{2,1,0:T(4,128)S(1)} %maximum_bitcast_fusion.1), channel_id=8, replica_groups=mesh['bz'=4,'by'=8,'bc'=2,'seq'=4,'mp'=2] {'by'}, dimensions={0}, use_global_device_ids=true | all-gather | bytes 55296 | tf_op jit(solution)/shard_map/all_gather | solution.py:42
  259.0 16.3 %all-gather.10 = f32[4,3,512]{2,1,0:T(4,128)S(1)} all-gather(f32[1,3,512]{2,1,0:T(4,128)S(1)} %maximum_bitcast_fusion.2), channel_id=9, replica_groups=mesh['bz'=4,'by'=8,'bc'=2,'seq'=4,'mp'=2] {'bz'}, dimensions={0}, use_global_device_ids=true | all-gather | bytes 30720 | tf_op jit(solution)/shard_map/all_gather | solution.py:42
  276.4 10.4 %all-reduce.7 = f32[32]{0:T(128)S(1)} all-reduce(f32[32]{0:T(128)S(1)} %convolution_bitcast_fusion.1), channel_id=12, replica_groups=mesh['bz'=4,'by'=8,'bc'=2,'seq'=4,'mp'=2] {'seq'}, use_global_device_ids=true, to_apply=%region_21.22.clone | all-reduce | flops 32 | bytes 256
  (106 shorter events, 13.4 us)
Async XLA Ops:
  7.2 220.9 %copy-start = (bf16[1536,786]{0,1:T(8,128)(2,1)S(1)}, bf16[1536,786]{0,1:T(8,128)(2,1)}, u32[]{:S(2)}) copy-start(bf16[1536,786]{0,1:T(8,128)(2,1)} %param.29) | copy-start | bytes 7243780
  7.2 49.1 %copy-start.14 = (s32[1,8]{1,0:T(1,128)S(1)}, s32[1,8]{1,0:T(1,128)}, u32[]{:S(2)}) copy-start(s32[1,8]{1,0:T(1,128)} %param.17) | copy-start | bytes 100
  7.2 49.4 %copy-start.5 = (bf16[48,1536]{1,0:T(8,128)(2,1)S(1)}, bf16[48,1536]{1,0:T(8,128)(2,1)}, u32[]{:S(2)}) copy-start(bf16[48,1536]{1,0:T(8,128)(2,1)} %param.27) | copy-start | bytes 442372
  7.2 51.9 %copy-start.1 = (f32[48]{0:T(128)S(1)}, f32[48]{0:T(128)}, u32[]{:S(2)}) copy-start(f32[48]{0:T(128)} %param.25) | copy-start | bytes 580
  7.2 53.4 %copy-start.10 = (f32[4,48]{1,0:T(4,128)S(1)}, f32[4,48]{1,0:T(4,128)}, u32[]{:S(2)}) copy-start(f32[4,48]{1,0:T(4,128)} %param.21) | copy-start | bytes 2308
  7.2 59.1 %copy-start.9 = (f32[4,256]{1,0:T(4,128)S(1)}, f32[4,256]{1,0:T(4,128)}, u32[]{:S(2)}) copy-start(f32[4,256]{1,0:T(4,128)} %param.22) | copy-start | bytes 12292
  7.2 65.1 %copy-start.4 = (bf16[1536,2,48]{0,2,1:T(8,128)(2,1)S(1)}, bf16[1536,2,48]{0,2,1:T(8,128)(2,1)}, u32[]{:S(2)}) copy-start(bf16[1536,2,48]{0,2,1:T(8,128)(2,1)} %param.19) | copy-start | bytes 884740
  7.2 65.1 %all-gather.14.cloned.1.call-start = ((), (), s32[]{:S(2)}) async-start(), calls=%async_computation.3 | async-start | bytes 2359296 | tf_op jit(solution)/shard_map/all_gather | solution.py:22
  56.2 79.8 %reduce-scatter.5.cloned.1.call-start = ((), (), s32[]{:S(2)}) async-start(), calls=%async_computation.2 | async-start | bytes 1916928 | tf_op jit(solution)/shard_map/reduce_scatter | solution.py:205
  72.3 2.2 copy-start.2
  74.5 2.6 copy-start.12
  74.5 2.6 copy-start.13
  76.4 0.7 copy-start.3
  81.3 1.5 copy-start.15
  92.3 76.6 %copy-start.7 = (bf16[1,8,1536]{2,1,0:T(8,128)(2,1)S(1)}, bf16[1,8,1536]{2,1,0:T(8,128)(2,1)}, u32[]{:S(2)}) copy-start(bf16[1,8,1536]{2,1,0:T(8,128)(2,1)} %param.15) | copy-start | bytes 73732
  92.3 77.7 %copy-start.8 = (f32[1536]{0:T(1024)S(1)}, f32[1536]{0:T(1024)}, u32[]{:S(2)}) copy-start(f32[1536]{0:T(1024)} %param.28) | copy-start | bytes 18436
  92.3 120.6 %copy-start.16 = (s32[32]{0:T(128)S(1)}, s32[32]{0:T(128)}, u32[]{:S(2)}) copy-start(s32[32]{0:T(128)} %param.18) | copy-start | bytes 388
  92.3 122.6 %copy-start.11 = (s32[1,512]{1,0:T(1,128)S(1)}, s32[1,512]{1,0:T(1,128)}, u32[]{:S(2)}) copy-start(s32[1,512]{1,0:T(1,128)} %param.16) | copy-start | bytes 6148
  92.4 75.8 %reduce-scatter.7.cloned.1.call-start = ((), (), s32[]{:S(2)}) async-start(), calls=%async_computation.5 | async-start | bytes 266240
  136.0 92.1 %all-gather.16.cloned.1.call-start = ((), (), s32[]{:S(2)}) async-start(), calls=%async_computation.4 | async-start | bytes 2359296 | tf_op jit(solution)/shard_map/all_gather | solution.py:22
  170.0 61.0 %copy-start.6 = (bf16[8,1536]{1,0:T(8,128)(2,1)}, bf16[8,1536]{1,0:T(8,128)(2,1)S(1)}, u32[]{:S(2)}) copy-start(bf16[8,1536]{1,0:T(8,128)(2,1)S(1)} %get-tuple-element.48) | copy-start | bytes 73732
Sparse Core Ops, SparseCore 0:
  56.3 15.9 all-gather.13
  92.5 43.4 reduce-scatter.4
  138.8 29.3 reduce-scatter.6
  213.1 14.9 all-gather.15

commit v5 on v4

--- a/solution.py
+++ b/solution.py
@@ -18,8 +18,7 @@
 
 def gather_rows(rows):
     part = lax.all_gather(rows, "bz", axis=0)
-    part = lax.all_gather(part, "by", axis=1)
-    part = lax.all_gather(part, "bc", axis=2)
+    part = lax.all_gather(part, ("by", "bc"), axis=1)
     return part.reshape((-1,) + rows.shape[1:])
 
 

time: 294 us -> 283 us (0.963)
  blocking collectives: 150 us -> 92.9 us
  waiting for transfers between devices: 94.9 us -> 135 us
    all_gather x2 -> x0, blocking collectives: 58.4 us -> none  [gather_rows(): part = lax.all_gather(part, 'by', axis=1)]
    all_gather x2, waiting for transfers between devices: 19.1 us -> 59.9 us  [gather_rows(): part = lax.all_gather(part, ('by', 'bc'), axis=1)]
  transfers between devices with their start and end apart: 4 -> 4, of which waited for: 4 -> 4; matrix products, arithmetic and copies ran while one was open for 3% -> 5% of each run, Pallas kernels for 0% -> 0%
where the time goes in v5:
time: 283 us; the launch traced here: 281 us
  waiting for transfers between devices  135 us (48%)
  blocking collectives  92.9 us (33%)
  between operations  14.8 us (5%)
  other arithmetic  13.7 us (5%)
  matrix products  13.1 us (5%)
  local copies, waits for them, and re-layouts  11.8 us (4%)
    all_gather x2, waiting for transfers between devices, gather_rows(): part = lax.all_gather(part, ('by', 'bc'), axis=1)  59.9 us
    all_gather x3, blocking collectives, combine_blk(): pieces = lax.all_gather(jnp.stack([top, expsum, target]), axis, axis=0)  42.6 us
    reduce_scatter x1, waiting for transfers between devices, shards(): packed = lax.psum_scatter(packed, 'by', scatter_dimension=0)  42.5 us
    all_gather x2, blocking collectives, gather_rows(): part = lax.all_gather(rows, 'bz', axis=0)  35.8 us
    unnamed x5, waiting for transfers between devices  32.3 us
    unnamed x1, blocking collectives  10.4 us
  transfers between devices with their start and end apart: 4, of which 4 were waited for; matrix products, arithmetic and copies ran while one was open for 5% of the time, Pallas kernels for 0%

profile of v5, /device:TPU:16, one launch (start us, length us, event | category | flops | bytes accessed | tf_op | source)
XLA Modules:
  0.0 281.3 jit_solution(5640339492771324845)
XLA Ops:
  7.2 21.3 %all_gather.45 = bf16[4,8,1536]{2,1,0:T(8,128)(2,1)} all-gather(bf16[1,8,1536]{2,1,0:T(8,128)(2,1)} %param.15), channel_id=1, replica_groups=mesh['bz'=4,'by'=8,'bc'=2,'seq'=4,'mp'=2] {'bz'}, dimensions={0}, use_global_device_ids=true | all-gather | bytes 122880 | tf_op jit(solution)/shard_map/all_gather | solution.py:20
  30.8 1.4 gather_fusion
  32.2 2.2 all_gather.49
  36.7 4.5 %compare_select_fusion.2 = s32[512,1]{0,1:T(1,128)S(1)} fusion(s32[]{:T(128)} %bitcast.12, s32[]{:T(128)} %bitcast.13, s32[]{:T(128)} %bitcast.14, s32[]{:T(128)} %bitcast.15, s32[]{:T(128)} %bitcast.16, s32[]{:T(128)} %bitcast.18, s32[]{:T(128)} %bitcast.17, s32[512,1]{0,1:T(1,128)S(1)} %bitcast.182, s32[512,1]{0,1:T(1,128)S(1)} %bitcast.180), kind=kLoop, calls=%fused_computation.101 | loop fusion | flops 7168 | bytes 6172 | tf_op jit(solution)/shard_map/jit(_take)/gather | solution.py:52
  41.1 1.3 compare_convert_fusion.4
  43.3 23.6 %all-gather.12.cloned.1.call-done = bf16[4,128,1536]{2,1,0:T(8,128)(2,1)} async-done(((bf16[4,8,1536]{2,1,0:T(8,128)(2,1)}), bf16[4,128,1536]{2,1,0:T(8,128)(2,1)}) %all-gather.12.cloned.1.call-update) | async-done | bytes 1572880 | tf_op jit(solution)/shard_map/all_gather | solution.py:21
  66.9 2.2 convolution_convert_fusion.1
  69.1 1.9 convolution_convert_fusion
  73.0 1.6 divide_multiply_fusion
  75.9 1.5 fusion.8
  77.4 1.5 multiply_convert_fusion
  80.3 2.0 all_gather.48
  83.0 1.5 fusion.27
  84.5 2.4 concatenate.43
  87.0 42.5 %reduce-scatter.5.cloned.1.call-done = f32[1,4,8,1664]{3,2,1,0:T(8,128)} async-done(((f32[8,4,8,1664]{3,2,1,0:T(8,128)}), f32[1,4,8,1664]{3,2,1,0:T(8,128)}) %reduce-scatter.5.cloned.1.call-update) | async-done | bytes 213008 | tf_op jit(solution)/shard_map/reduce_scatter | solution.py:204
  129.6 32.3 %reduce-scatter.7.cloned.1.call-done = f32[1,8,1664]{2,1,0:T(8,128)} async-done(((f32[4,8,1664]{2,1,0:T(8,128)}), f32[1,8,1664]{2,1,0:T(8,128)}) %reduce-scatter.7.cloned.1.call-update) | async-done | bytes 53264
  163.8 14.5 %all-gather.1 = bf16[32,1536]{1,0:T(8,128)(2,1)} all-gather(bf16[8,1536]{1,0:T(8,128)(2,1)S(1)} %fusion.41), channel_id=3, replica_groups=mesh['bz'=4,'by'=8,'bc'=2,'seq'=4,'mp'=2] {'bz'}, dimensions={0}, use_global_device_ids=true | all-gather | bytes 122880 | tf_op jit(solution)/shard_map/all_gather | solution.py:20
  178.4 1.3 dynamic-slice.7
  180.3 36.3 %all-gather.14.cloned.1.call-done = bf16[4,128,1536]{2,1,0:T(8,128)(2,1)} async-done(((bf16[4,8,1536]{2,1,0:T(8,128)(2,1)}), bf16[4,128,1536]{2,1,0:T(8,128)(2,1)}) %all-gather.14.cloned.1.call-update) | async-done | bytes 1572880 | tf_op jit(solution)/shard_map/all_gather | solution.py:21
  216.6 2.9 %fusion.81 = (f32[512]{0:T(512)S(1)}, f32[512,786]{0,1:T(8,128)S(1)}) fusion(bf16[512,1536]{1,0:T(8,128)(2,1)} %bitcast.208, bf16[1536,786]{0,1:T(8,128)(2,1)S(1)} %copy-done), kind=kOutput, calls=%fused_computation.175 | convolution fusion | flops 1236673024 | bytes 5599232 | tf_op jit(solution)/shard_map/dot_general | solution.py:209
  219.9 1.8 all-gather.6
  221.8 24.5 %all-gather.7 = f32[8,3,512]{2,1,0:T(4,128)S(1)} all-gather(f32[1,3,512]{2,1,0:T(4,128)S(1)} %maximum_bitcast_fusion.1), channel_id=6, replica_groups=mesh['bz'=4,'by'=8,'bc'=2,'seq'=4,'mp'=2] {'by'}, dimensions={0}, use_global_device_ids=true | all-gather | bytes 55296 | tf_op jit(solution)/shard_map/all_gather | solution.py:41
  246.4 16.3 %all-gather.8 = f32[4,3,512]{2,1,0:T(4,128)S(1)} all-gather(f32[1,3,512]{2,1,0:T(4,128)S(1)} %maximum_bitcast_fusion.2), channel_id=7, replica_groups=mesh['bz'=4,'by'=8,'bc'=2,'seq'=4,'mp'=2] {'bz'}, dimensions={0}, use_global_device_ids=true | all-gather | bytes 30720 | tf_op jit(solution)/shard_map/all_gather | solution.py:41
  263.8 10.4 %all-reduce.7 = f32[32]{0:T(128)S(1)} all-reduce(f32[32]{0:T(128)S(1)} %convolution_bitcast_fusion.1), channel_id=10, replica_groups=mesh['bz'=4,'by'=8,'bc'=2,'seq'=4,'mp'=2] {'seq'}, use_global_device_ids=true, to_apply=%region_21.22.clone | all-reduce | flops 32 | bytes 256
  (93 shorter events, 15.1 us)
Async XLA Ops:
  7.2 209.4 %copy-start = (bf16[1536,786]{0,1:T(8,128)(2,1)S(1)}, bf16[1536,786]{0,1:T(8,128)(2,1)}, u32[]{:S(2)}) copy-start(bf16[1536,786]{0,1:T(8,128)(2,1)} %param.29) | copy-start | bytes 7243780
  7.2 59.7 %all-gather.12.cloned.1.call-start = ((), (), s32[]{:S(2)}) async-start(), calls=%async_computation.3 | async-start | bytes 1671168 | tf_op jit(solution)/shard_map/all_gather | solution.py:21
  28.6 101.0 %reduce-scatter.5.cloned.1.call-start = ((), (), s32[]{:S(2)}) async-start(), calls=%async_computation.2 | async-start | bytes 1916928 | tf_op jit(solution)/shard_map/reduce_scatter | solution.py:204
  66.9 2.2 copy-start.1
  69.1 2.6 copy-start.7
  69.1 2.6 copy-start.8
  71.0 0.7 copy-start.2
  75.9 1.5 copy-start.9
  87.0 75.7 %copy-start.4 = (bf16[1,8,1536]{2,1,0:T(8,128)(2,1)S(1)}, bf16[1,8,1536]{2,1,0:T(8,128)(2,1)}, u32[]{:S(2)}) copy-start(bf16[1,8,1536]{2,1,0:T(8,128)(2,1)} %param.15) | copy-start | bytes 73732
  87.0 76.8 %copy-start.5 = (f32[1536]{0:T(1024)S(1)}, f32[1536]{0:T(1024)}, u32[]{:S(2)}) copy-start(f32[1536]{0:T(1024)} %param.28) | copy-start | bytes 18436
  87.0 91.3 %copy-start.10 = (s32[32]{0:T(128)S(1)}, s32[32]{0:T(128)}, u32[]{:S(2)}) copy-start(s32[32]{0:T(128)} %param.18) | copy-start | bytes 388
  87.0 93.3 %copy-start.6 = (s32[1,512]{1,0:T(1,128)S(1)}, s32[1,512]{1,0:T(1,128)}, u32[]{:S(2)}) copy-start(s32[1,512]{1,0:T(1,128)} %param.16) | copy-start | bytes 6148
  87.0 74.9 %reduce-scatter.7.cloned.1.call-start = ((), (), s32[]{:S(2)}) async-start(), calls=%async_computation.5 | async-start | bytes 266240
  129.6 87.0 %all-gather.14.cloned.1.call-start = ((), (), s32[]{:S(2)}) async-start(), calls=%async_computation.4 | async-start | bytes 1671168 | tf_op jit(solution)/shard_map/all_gather | solution.py:21
  163.7 55.8 %copy-start.3 = (bf16[8,1536]{1,0:T(8,128)(2,1)}, bf16[8,1536]{1,0:T(8,128)(2,1)S(1)}, u32[]{:S(2)}) copy-start(bf16[8,1536]{1,0:T(8,128)(2,1)S(1)} %get-tuple-element.48) | copy-start | bytes 73732
Sparse Core Ops, SparseCore 0:
  28.7 38.1 all-gather.11
  87.1 42.4 reduce-scatter.4
  132.4 29.4 reduce-scatter.6
  178.4 38.1 all-gather.13

commit v6 on v5

--- a/solution.py
+++ b/solution.py
@@ -200,8 +200,8 @@
     packed = jnp.concatenate(
         [partial, squares_pair[:, None], jnp.zeros((half_rows, 127), jnp.float32)], axis=1
     )
-    packed = packed.reshape(by, bz, rows_count, D + 128)
-    packed = lax.psum_scatter(packed, "by", scatter_dimension=0)
+    packed = packed.reshape(by, bz, rows_count, D + 128).astype(jnp.bfloat16)
+    packed = lax.psum_scatter(packed, "by", scatter_dimension=0).astype(jnp.float32)
     packed_own = lax.psum_scatter(packed, "bz", scatter_dimension=0)
     inverse = lax.rsqrt(packed_own[:, D] / inner_total + EPSILON)
     delta_own = packed_own[:, :D] * inverse[:, None]

time: 283 us -> 281 us (level)
  waiting for transfers between devices: 135 us -> 130 us
where the time goes in v6:
time: 281 us; the launch traced here: 279 us
  waiting for transfers between devices  130 us (46%)
  blocking collectives  92.9 us (33%)
  other arithmetic  15.3 us (5%)
  between operations  14.9 us (5%)
  matrix products  12.8 us (5%)
  local copies, waits for them, and re-layouts  12.5 us (4%)
    all_gather x2, waiting for transfers between devices, gather_rows(): part = lax.all_gather(part, ('by', 'bc'), axis=1)  59.9 us
    all_gather x3, blocking collectives, combine_blk(): pieces = lax.all_gather(jnp.stack([top, expsum, target]), axis, axis=0)  42.6 us
    reduce_scatter x1, waiting for transfers between devices, shards(): lax.psum_scatter(packed, 'by', scatter_dimension=0).astype(jnp.float32)  40 us
    all_gather x2, blocking collectives, gather_rows(): part = lax.all_gather(rows, 'bz', axis=0)  35.8 us
    unnamed x5, waiting for transfers between devices  30.7 us
    unnamed x1, blocking collectives  10.4 us
  transfers between devices with their start and end apart: 4, of which 4 were waited for; matrix products, arithmetic and copies ran while one was open for 5% of the time, Pallas kernels for 0%

profile of v6, /device:TPU:16, one launch (start us, length us, event | category | flops | bytes accessed | tf_op | source)
XLA Modules:
  0.0 279.0 jit_solution(9529156022673650317)
XLA Ops:
  7.2 21.3 %all_gather.45 = bf16[4,8,1536]{2,1,0:T(8,128)(2,1)} all-gather(bf16[1,8,1536]{2,1,0:T(8,128)(2,1)} %param.15), channel_id=1, replica_groups=mesh['bz'=4,'by'=8,'bc'=2,'seq'=4,'mp'=2] {'bz'}, dimensions={0}, use_global_device_ids=true | all-gather | bytes 122880 | tf_op jit(solution)/shard_map/all_gather | solution.py:20
  30.8 1.4 gather_fusion
  32.2 2.2 all_gather.49
  36.7 4.5 %compare_select_fusion.2 = s32[512,1]{0,1:T(1,128)S(1)} fusion(s32[]{:T(128)} %bitcast.12, s32[]{:T(128)} %bitcast.13, s32[]{:T(128)} %bitcast.14, s32[]{:T(128)} %bitcast.15, s32[]{:T(128)} %bitcast.16, s32[]{:T(128)} %bitcast.18, s32[]{:T(128)} %bitcast.17, s32[512,1]{0,1:T(1,128)S(1)} %bitcast.183, s32[512,1]{0,1:T(1,128)S(1)} %bitcast.181), kind=kLoop, calls=%fused_computation.102 | loop fusion | flops 7168 | bytes 6172 | tf_op jit(solution)/shard_map/jit(_take)/gather | solution.py:52
  41.1 1.3 compare_convert_fusion.4
  43.3 23.6 %all-gather.12.cloned.1.call-done = bf16[4,128,1536]{2,1,0:T(8,128)(2,1)} async-done(((bf16[4,8,1536]{2,1,0:T(8,128)(2,1)}), bf16[4,128,1536]{2,1,0:T(8,128)(2,1)}) %all-gather.12.cloned.1.call-update) | async-done | bytes 1572880 | tf_op jit(solution)/shard_map/all_gather | solution.py:21
  66.9 2.2 convolution_convert_fusion.2
  69.1 1.9 convolution_convert_fusion.1
  73.0 1.6 divide_multiply_fusion
  75.9 1.5 fusion.8
  77.4 1.5 multiply_convert_fusion
  80.2 2.0 all_gather.48
  85.5 1.8 concatenate.44
  87.4 40.0 %reduce-scatter.5.cloned.1.call-done = bf16[1,4,8,1664]{3,2,1,0:T(8,128)(2,1)} async-done(((bf16[8,4,8,1664]{3,2,1,0:T(8,128)(2,1)}), bf16[1,4,8,1664]{3,2,1,0:T(8,128)(2,1)}) %reduce-scatter.5.cloned.1.call-update) | async-done | bytes 106512 | tf_op jit(solution)/shard_map/reduce_scatter | solution.py:204
  127.3 1.6 bitcast_convert_fusion
  129.0 30.6 %reduce-scatter.7.cloned.1.call-done = f32[1,8,1664]{2,1,0:T(8,128)} async-done(((f32[4,8,1664]{2,1,0:T(8,128)}), f32[1,8,1664]{2,1,0:T(8,128)}) %reduce-scatter.7.cloned.1.call-update) | async-done | bytes 53264
  161.5 14.5 %all-gather.1 = bf16[32,1536]{1,0:T(8,128)(2,1)} all-gather(bf16[8,1536]{1,0:T(8,128)(2,1)S(1)} %fusion.40), channel_id=3, replica_groups=mesh['bz'=4,'by'=8,'bc'=2,'seq'=4,'mp'=2] {'bz'}, dimensions={0}, use_global_device_ids=true | all-gather | bytes 122880 | tf_op jit(solution)/shard_map/all_gather | solution.py:20
  176.1 1.3 dynamic-slice.7
  178.0 36.3 %all-gather.14.cloned.1.call-done = bf16[4,128,1536]{2,1,0:T(8,128)(2,1)} async-done(((bf16[4,8,1536]{2,1,0:T(8,128)(2,1)}), bf16[4,128,1536]{2,1,0:T(8,128)(2,1)}) %all-gather.14.cloned.1.call-update) | async-done | bytes 1572880 | tf_op jit(solution)/shard_map/all_gather | solution.py:21
  214.3 2.9 %fusion.80 = (f32[512]{0:T(512)S(1)}, f32[512,786]{0,1:T(8,128)S(1)}) fusion(bf16[512,1536]{1,0:T(8,128)(2,1)} %bitcast.209, bf16[1536,786]{0,1:T(8,128)(2,1)S(1)} %copy-done), kind=kOutput, calls=%fused_computation.176 | convolution fusion | flops 1236673024 | bytes 5599232 | tf_op jit(solution)/shard_map/dot_general | solution.py:209
  217.6 1.8 all-gather.6
  219.5 24.5 %all-gather.7 = f32[8,3,512]{2,1,0:T(4,128)S(1)} all-gather(f32[1,3,512]{2,1,0:T(4,128)S(1)} %maximum_bitcast_fusion.1), channel_id=6, replica_groups=mesh['bz'=4,'by'=8,'bc'=2,'seq'=4,'mp'=2] {'by'}, dimensions={0}, use_global_device_ids=true | all-gather | bytes 55296 | tf_op jit(solution)/shard_map/all_gather | solution.py:41
  244.1 16.3 %all-gather.8 = f32[4,3,512]{2,1,0:T(4,128)S(1)} all-gather(f32[1,3,512]{2,1,0:T(4,128)S(1)} %maximum_bitcast_fusion.2), channel_id=7, replica_groups=mesh['bz'=4,'by'=8,'bc'=2,'seq'=4,'mp'=2] {'bz'}, dimensions={0}, use_global_device_ids=true | all-gather | bytes 30720 | tf_op jit(solution)/shard_map/all_gather | solution.py:41
  261.5 10.4 %all-reduce.7 = f32[32]{0:T(128)S(1)} all-reduce(f32[32]{0:T(128)S(1)} %convolution_bitcast_fusion.1), channel_id=10, replica_groups=mesh['bz'=4,'by'=8,'bc'=2,'seq'=4,'mp'=2] {'seq'}, use_global_device_ids=true, to_apply=%region_21.22.clone | all-reduce | flops 32 | bytes 256
  (94 shorter events, 17.5 us)
Async XLA Ops:
  7.2 207.1 %copy-start = (bf16[1536,786]{0,1:T(8,128)(2,1)S(1)}, bf16[1536,786]{0,1:T(8,128)(2,1)}, u32[]{:S(2)}) copy-start(bf16[1536,786]{0,1:T(8,128)(2,1)} %param.29) | copy-start | bytes 7243780
  7.2 59.7 %all-gather.12.cloned.1.call-start = ((), (), s32[]{:S(2)}) async-start(), calls=%async_computation.3 | async-start | bytes 1671168 | tf_op jit(solution)/shard_map/all_gather | solution.py:21
  28.6 98.8 %reduce-scatter.5.cloned.1.call-start = ((), (), s32[]{:S(2)}) async-start(), calls=%async_computation.2 | async-start | bytes 958464 | tf_op jit(solution)/shard_map/reduce_scatter | solution.py:204
  66.9 2.2 copy-start.1
  69.1 2.6 copy-start.7
  69.1 2.6 copy-start.8
  71.0 0.7 copy-start.2
  75.9 1.5 copy-start.9
  85.4 74.9 %copy-start.4 = (bf16[1,8,1536]{2,1,0:T(8,128)(2,1)S(1)}, bf16[1,8,1536]{2,1,0:T(8,128)(2,1)}, u32[]{:S(2)}) copy-start(bf16[1,8,1536]{2,1,0:T(8,128)(2,1)} %param.15) | copy-start | bytes 73732
  85.5 75.9 %copy-start.5 = (f32[1536]{0:T(1024)S(1)}, f32[1536]{0:T(1024)}, u32[]{:S(2)}) copy-start(f32[1536]{0:T(1024)} %param.28) | copy-start | bytes 18436
  85.5 90.5 %copy-start.10 = (s32[32]{0:T(128)S(1)}, s32[32]{0:T(128)}, u32[]{:S(2)}) copy-start(s32[32]{0:T(128)} %param.18) | copy-start | bytes 388
  85.5 92.5 %copy-start.6 = (s32[1,512]{1,0:T(1,128)S(1)}, s32[1,512]{1,0:T(1,128)}, u32[]{:S(2)}) copy-start(s32[1,512]{1,0:T(1,128)} %param.16) | copy-start | bytes 6148
  87.3 72.3 %reduce-scatter.7.cloned.1.call-start = ((), (), s32[]{:S(2)}) async-start(), calls=%async_computation.5 | async-start | bytes 266240
  128.9 85.3 %all-gather.14.cloned.1.call-start = ((), (), s32[]{:S(2)}) async-start(), calls=%async_computation.4 | async-start | bytes 1671168 | tf_op jit(solution)/shard_map/all_gather | solution.py:21
  161.4 55.8 %copy-start.3 = (bf16[8,1536]{1,0:T(8,128)(2,1)}, bf16[8,1536]{1,0:T(8,128)(2,1)S(1)}, u32[]{:S(2)}) copy-start(bf16[8,1536]{1,0:T(8,128)(2,1)S(1)} %get-tuple-element.48) | copy-start | bytes 73732
Sparse Core Ops, SparseCore 0:
  28.7 38.1 all-gather.11
  87.4 39.8 reduce-scatter.4
  130.1 29.3 reduce-scatter.6
  176.1 38.1 all-gather.13

commit v7 on v5

--- a/solution.py
+++ b/solution.py
@@ -37,7 +37,7 @@
 
 
 def combine_blk(top, expsum, target):
-    for axis in ("bc", "by", "bz"):
+    for axis in (("by", "bc"), "bz"):
         pieces = lax.all_gather(jnp.stack([top, expsum, target]), axis, axis=0)
         top = jnp.max(pieces[:, 0], axis=0)
         expsum = jnp.sum(pieces[:, 1] * jnp.exp(pieces[:, 0] - top[None]), axis=0)

time: 283 us -> 272 us (0.961)
  the two profiles are of different devices: /device:TPU:16 before, /device:TPU:8 now
where the time goes in v7:
time: 272 us; the launch traced here: 271 us
  waiting for transfers between devices  136 us (50%)
  blocking collectives  81.9 us (30%)
  between operations  14.8 us (5%)
  other arithmetic  13.7 us (5%)
  matrix products  13.1 us (5%)
  local copies, waits for them, and re-layouts  11.8 us (4%)
    all_gather x2, waiting for transfers between devices, gather_rows(): part = lax.all_gather(part, ('by', 'bc'), axis=1)  62 us
    reduce_scatter x1, waiting for transfers between devices, shards(): packed = lax.psum_scatter(packed, 'by', scatter_dimension=0)  42.5 us
    all_gather x2, blocking collectives, gather_rows(): part = lax.all_gather(rows, 'bz', axis=0)  35.8 us
    all_gather x2, blocking collectives, combine_blk(): pieces = lax.all_gather(jnp.stack([top, expsum, target]), axis, axis=0)  31.5 us
    unnamed x5, waiting for transfers between devices  31.3 us
    unnamed x1, blocking collectives  10.4 us
  transfers between devices with their start and end apart: 4, of which 4 were waited for; matrix products, arithmetic and copies ran while one was open for 5% of the time, Pallas kernels for 0%

profile of v7, /device:TPU:8, one launch (start us, length us, event | category | flops | bytes accessed | tf_op | source)
XLA Modules:
  0.0 271.4 jit_solution(8301393565326534743)
XLA Ops:
  7.2 21.3 %all_gather.39 = bf16[4,8,1536]{2,1,0:T(8,128)(2,1)} all-gather(bf16[1,8,1536]{2,1,0:T(8,128)(2,1)} %param.15), channel_id=1, replica_groups=mesh['bz'=4,'by'=8,'bc'=2,'seq'=4,'mp'=2] {'bz'}, dimensions={0}, use_global_device_ids=true | all-gather | bytes 122880 | tf_op jit(solution)/shard_map/all_gather | solution.py:20
  30.8 1.4 gather_fusion
  32.2 2.2 all_gather.43
  36.7 4.5 %compare_select_fusion.2 = s32[512,1]{0,1:T(1,128)S(1)} fusion(s32[]{:T(128)} %bitcast.12, s32[]{:T(128)} %bitcast.13, s32[]{:T(128)} %bitcast.14, s32[]{:T(128)} %bitcast.15, s32[]{:T(128)} %bitcast.16, s32[]{:T(128)} %bitcast.18, s32[]{:T(128)} %bitcast.17, s32[512,1]{0,1:T(1,128)S(1)} %bitcast.163, s32[512,1]{0,1:T(1,128)S(1)} %bitcast.161), kind=kLoop, calls=%fused_computation.100 | loop fusion | flops 7168 | bytes 6172 | tf_op jit(solution)/shard_map/jit(_take)/gather | solution.py:52
  41.1 1.3 compare_convert_fusion.4
  43.3 24.7 %all-gather.10.cloned.1.call-done = bf16[4,128,1536]{2,1,0:T(8,128)(2,1)} async-done(((bf16[4,8,1536]{2,1,0:T(8,128)(2,1)}), bf16[4,128,1536]{2,1,0:T(8,128)(2,1)}) %all-gather.10.cloned.1.call-update) | async-done | bytes 1572880 | tf_op jit(solution)/shard_map/all_gather | solution.py:21
  68.0 2.2 convolution_convert_fusion.1
  70.2 1.9 convolution_convert_fusion
  74.1 1.6 divide_multiply_fusion
  75.7 1.0 fusion.29
  77.0 1.5 fusion.8
  78.5 1.5 multiply_convert_fusion
  81.4 2.0 all_gather.42
  84.1 1.5 fusion.27
  85.6 2.4 concatenate.43
  88.2 42.5 %reduce-scatter.5.cloned.1.call-done = f32[1,4,8,1664]{3,2,1,0:T(8,128)} async-done(((f32[8,4,8,1664]{3,2,1,0:T(8,128)}), f32[1,4,8,1664]{3,2,1,0:T(8,128)}) %reduce-scatter.5.cloned.1.call-update) | async-done | bytes 213008 | tf_op jit(solution)/shard_map/reduce_scatter | solution.py:204
  130.7 31.2 %reduce-scatter.7.cloned.1.call-done = f32[1,8,1664]{2,1,0:T(8,128)} async-done(((f32[4,8,1664]{2,1,0:T(8,128)}), f32[1,8,1664]{2,1,0:T(8,128)}) %reduce-scatter.7.cloned.1.call-update) | async-done | bytes 53264
  163.9 14.5 %all-gather.1 = bf16[32,1536]{1,0:T(8,128)(2,1)} all-gather(bf16[8,1536]{1,0:T(8,128)(2,1)S(1)} %fusion.41), channel_id=3, replica_groups=mesh['bz'=4,'by'=8,'bc'=2,'seq'=4,'mp'=2] {'bz'}, dimensions={0}, use_global_device_ids=true | all-gather | bytes 122880 | tf_op jit(solution)/shard_map/all_gather | solution.py:20
  178.5 1.3 dynamic-slice.7
  180.4 37.3 %all-gather.12.cloned.1.call-done = bf16[4,128,1536]{2,1,0:T(8,128)(2,1)} async-done(((bf16[4,8,1536]{2,1,0:T(8,128)(2,1)}), bf16[4,128,1536]{2,1,0:T(8,128)(2,1)}) %all-gather.12.cloned.1.call-update) | async-done | bytes 1572880 | tf_op jit(solution)/shard_map/all_gather | solution.py:21
  217.7 2.9 %fusion.76 = (f32[512]{0:T(512)S(1)}, f32[512,786]{0,1:T(8,128)S(1)}) fusion(bf16[512,1536]{1,0:T(8,128)(2,1)} %bitcast.186, bf16[1536,786]{0,1:T(8,128)(2,1)S(1)} %copy-done), kind=kOutput, calls=%fused_computation.166 | convolution fusion | flops 1236673024 | bytes 5599232 | tf_op jit(solution)/shard_map/dot_general | solution.py:209
  221.0 15.3 %all-gather.5 = f32[16,3,512]{2,1,0:T(4,128)S(1)} all-gather(f32[1,3,512]{2,1,0:T(4,128)S(1)} %maximum_bitcast_fusion), channel_id=5, replica_groups=mesh['bz'=4,'by'=8,'bc'=2,'seq'=4,'mp'=2] {'by','bc'}, dimensions={0}, use_global_device_ids=true | all-gather | bytes 104448 | tf_op jit(solution)/shard_map/all_gather | solution.py:41
  236.4 16.3 %all-gather.6 = f32[4,3,512]{2,1,0:T(4,128)S(1)} all-gather(f32[1,3,512]{2,1,0:T(4,128)S(1)} %maximum_bitcast_fusion.1), channel_id=6, replica_groups=mesh['bz'=4,'by'=8,'bc'=2,'seq'=4,'mp'=2] {'bz'}, dimensions={0}, use_global_device_ids=true | all-gather | bytes 30720 | tf_op jit(solution)/shard_map/all_gather | solution.py:41
  253.8 10.4 %all-reduce.7 = f32[32]{0:T(128)S(1)} all-reduce(f32[32]{0:T(128)S(1)} %convolution_bitcast_fusion.1), channel_id=9, replica_groups=mesh['bz'=4,'by'=8,'bc'=2,'seq'=4,'mp'=2] {'seq'}, use_global_device_ids=true, to_apply=%region_18.19.clone | all-reduce | flops 32 | bytes 256
  (89 shorter events, 14.0 us)
Async XLA Ops:
  7.2 210.5 %copy-start = (bf16[1536,786]{0,1:T(8,128)(2,1)S(1)}, bf16[1536,786]{0,1:T(8,128)(2,1)}, u32[]{:S(2)}) copy-start(bf16[1536,786]{0,1:T(8,128)(2,1)} %param.29) | copy-start | bytes 7243780
  7.2 60.8 %all-gather.10.cloned.1.call-start = ((), (), s32[]{:S(2)}) async-start(), calls=%async_computation.3 | async-start | bytes 1671168 | tf_op jit(solution)/shard_map/all_gather | solution.py:21
  28.6 102.1 %reduce-scatter.5.cloned.1.call-start = ((), (), s32[]{:S(2)}) async-start(), calls=%async_computation.2 | async-start | bytes 1916928 | tf_op jit(solution)/shard_map/reduce_scatter | solution.py:204
  68.0 2.2 copy-start.1
  70.2 2.6 copy-start.7
  70.2 2.6 copy-start.8
  72.1 0.7 copy-start.2
  77.0 1.5 copy-start.9
  88.1 74.7 %copy-start.4 = (bf16[1,8,1536]{2,1,0:T(8,128)(2,1)S(1)}, bf16[1,8,1536]{2,1,0:T(8,128)(2,1)}, u32[]{:S(2)}) copy-start(bf16[1,8,1536]{2,1,0:T(8,128)(2,1)} %param.15) | copy-start | bytes 73732
  88.1 75.7 %copy-start.5 = (f32[1536]{0:T(1024)S(1)}, f32[1536]{0:T(1024)}, u32[]{:S(2)}) copy-start(f32[1536]{0:T(1024)} %param.28) | copy-start | bytes 18436
  88.1 90.3 %copy-start.10 = (s32[32]{0:T(128)S(1)}, s32[32]{0:T(128)}, u32[]{:S(2)}) copy-start(s32[32]{0:T(128)} %param.18) | copy-start | bytes 388
  88.1 92.3 %copy-start.6 = (s32[1,512]{1,0:T(1,128)S(1)}, s32[1,512]{1,0:T(1,128)}, u32[]{:S(2)}) copy-start(s32[1,512]{1,0:T(1,128)} %param.16) | copy-start | bytes 6148
  88.1 73.9 %reduce-scatter.7.cloned.1.call-start = ((), (), s32[]{:S(2)}) async-start(), calls=%async_computation.5 | async-start | bytes 266240
  130.7 87.0 %all-gather.12.cloned.1.call-start = ((), (), s32[]{:S(2)}) async-start(), calls=%async_computation.4 | async-start | bytes 1671168 | tf_op jit(solution)/shard_map/all_gather | solution.py:21
  163.8 56.8 %copy-start.3 = (bf16[8,1536]{1,0:T(8,128)(2,1)}, bf16[8,1536]{1,0:T(8,128)(2,1)S(1)}, u32[]{:S(2)}) copy-start(bf16[8,1536]{1,0:T(8,128)(2,1)S(1)} %get-tuple-element.34) | copy-start | bytes 73732
Sparse Core Ops, SparseCore 0:
  28.7 39.2 all-gather.9
  88.2 42.3 reduce-scatter.4
  133.5 28.4 reduce-scatter.6
  178.5 39.1 all-gather.11

commit v8 on v7

--- a/solution.py
+++ b/solution.py
@@ -37,7 +37,7 @@
 
 
 def combine_blk(top, expsum, target):
-    for axis in (("by", "bc"), "bz"):
+    for axis in (("bz", "by", "bc"),):
         pieces = lax.all_gather(jnp.stack([top, expsum, target]), axis, axis=0)
         top = jnp.max(pieces[:, 0], axis=0)
         expsum = jnp.sum(pieces[:, 1] * jnp.exp(pieces[:, 0] - top[None]), axis=0)

time: 272 us -> 323 us (1.19)
  the two profiles are of different devices: /device:TPU:8 before, /device:TPU:1 now
where the time goes in v8:
time: 323 us
  waiting for transfers between devices  139 us (43%)
  blocking collectives  130 us (40%)
  between operations  14.8 us (5%)
  other arithmetic  13.8 us (4%)
  matrix products  13.1 us (4%)
  local copies, waits for them, and re-layouts  11.8 us (4%)
    all_gather x1, blocking collectives, combine_blk(): pieces = lax.all_gather(jnp.stack([top, expsum, target]), axis, axis=0)  83.3 us
    all_gather x2, waiting for transfers between devices, gather_rows(): part = lax.all_gather(part, ('by', 'bc'), axis=1)  68.2 us
    reduce_scatter x1, waiting for transfers between devices, shards(): packed = lax.psum_scatter(packed, 'by', scatter_dimension=0)  38.4 us
    unnamed x5, waiting for transfers between devices  32.5 us
    all_gather x2, blocking collectives, gather_rows(): part = lax.all_gather(rows, 'bz', axis=0)  30.8 us
    unnamed x1, blocking collectives  8.4 us
  transfers between devices with their start and end apart: 4, of which 4 were waited for; matrix products, arithmetic and copies ran while one was open for 4% of the time, Pallas kernels for 0%

profile of v8, /device:TPU:1, one launch (start us, length us, event | category | flops | bytes accessed | tf_op | source)
XLA Modules:
  0.0 322.9 jit_solution(2496920018480573930)
XLA Ops:
  7.2 19.3 %all_gather.33 = bf16[4,8,1536]{2,1,0:T(8,128)(2,1)} all-gather(bf16[1,8,1536]{2,1,0:T(8,128)(2,1)} %param.15), channel_id=1, replica_groups=mesh['bz'=4,'by'=8,'bc'=2,'seq'=4,'mp'=2] {'bz'}, dimensions={0}, use_global_device_ids=true | all-gather | bytes 122880 | tf_op jit(solution)/shard_map/all_gather | solution.py:20
  28.7 1.4 gather_fusion
  30.2 5.4 %all_gather.37 = bf16[96,1536]{1,0:T(8,128)(2,1)S(1)} all-gather(bf16[48,1536]{1,0:T(8,128)(2,1)} %param.27), channel_id=1, replica_groups=mesh['bz'=4,'by'=8,'bc'=2,'seq'=4,'mp'=2] {'bc'}, dimensions={0}, use_global_device_ids=true | all-gather | bytes 442368 | tf_op jit(solution)/shard_map/all_gather | solution.py:198
  37.8 4.5 %compare_select_fusion.2 = s32[512,1]{0,1:T(1,128)S(1)} fusion(s32[]{:T(128)} %bitcast.12, s32[]{:T(128)} %bitcast.13, s32[]{:T(128)} %bitcast.14, s32[]{:T(128)} %bitcast.15, s32[]{:T(128)} %bitcast.16, s32[]{:T(128)} %bitcast.18, s32[]{:T(128)} %bitcast.17, s32[512,1]{0,1:T(1,128)S(1)} %bitcast.145, s32[512,1]{0,1:T(1,128)S(1)} %bitcast.143), kind=kLoop, calls=%fused_computation.93 | loop fusion | flops 7168 | bytes 6172 | tf_op jit(solution)/shard_map/jit(_take)/gather | solution.py:52
  42.3 1.3 compare_convert_fusion.4
  44.4 25.2 %all-gather.8.cloned.1.call-done = bf16[4,128,1536]{2,1,0:T(8,128)(2,1)} async-done(((bf16[4,8,1536]{2,1,0:T(8,128)(2,1)}), bf16[4,128,1536]{2,1,0:T(8,128)(2,1)}) %all-gather.8.cloned.1.call-update) | async-done | bytes 1572880 | tf_op jit(solution)/shard_map/all_gather | solution.py:21
  69.6 2.2 convolution_convert_fusion.1
  71.8 1.9 convolution_convert_fusion
  75.6 1.6 divide_multiply_fusion
  77.3 1.0 fusion.29
  78.6 1.5 fusion.8
  80.1 1.5 multiply_convert_fusion
  82.9 2.0 all_gather.36
  85.7 1.5 fusion.27
  87.2 2.4 concatenate.43
  89.7 38.4 %reduce-scatter.5.cloned.1.call-done = f32[1,4,8,1664]{3,2,1,0:T(8,128)} async-done(((f32[8,4,8,1664]{3,2,1,0:T(8,128)}), f32[1,4,8,1664]{3,2,1,0:T(8,128)}) %reduce-scatter.5.cloned.1.call-update) | async-done | bytes 213008 | tf_op jit(solution)/shard_map/reduce_scatter | solution.py:204
  128.2 32.4 %reduce-scatter.7.cloned.1.call-done = f32[1,8,1664]{2,1,0:T(8,128)} async-done(((f32[4,8,1664]{2,1,0:T(8,128)}), f32[1,8,1664]{2,1,0:T(8,128)}) %reduce-scatter.7.cloned.1.call-update) | async-done | bytes 53264
  161.4 1.0 fusion.42
  162.5 11.6 %all-gather.1 = bf16[32,1536]{1,0:T(8,128)(2,1)} all-gather(bf16[8,1536]{1,0:T(8,128)(2,1)S(1)} %fusion.44), channel_id=3, replica_groups=mesh['bz'=4,'by'=8,'bc'=2,'seq'=4,'mp'=2] {'bz'}, dimensions={0}, use_global_device_ids=true | all-gather | bytes 122880 | tf_op jit(solution)/shard_map/all_gather | solution.py:20
  174.2 1.3 dynamic-slice.7
  176.2 43.1 %all-gather.10.cloned.1.call-done = bf16[4,128,1536]{2,1,0:T(8,128)(2,1)} async-done(((bf16[4,8,1536]{2,1,0:T(8,128)(2,1)}), bf16[4,128,1536]{2,1,0:T(8,128)(2,1)}) %all-gather.10.cloned.1.call-update) | async-done | bytes 1572880 | tf_op jit(solution)/shard_map/all_gather | solution.py:21
  219.3 2.9 fusion.71
  222.6 83.3 %all-gather.4 = f32[64,3,512]{2,1,0:T(4,128)S(1)} all-gather(f32[1,3,512]{2,1,0:T(4,128)S(1)} %maximum_bitcast_fusion), channel_id=5, replica_groups=mesh['bz'=4,'by'=8,'bc'=2,'seq'=4,'mp'=2] {'bz','by','bc'}, dimensions={0}, use_global_device_ids=true | all-gather | bytes 399360 | tf_op jit(solution)/shard_map/all_gather | solution.py:41
  307.4 8.4 %all-reduce.7 = f32[32]{0:T(128)S(1)} all-reduce(f32[32]{0:T(128)S(1)} %convolution_bitcast_fusion.1), channel_id=8, replica_groups=mesh['bz'=4,'by'=8,'bc'=2,'seq'=4,'mp'=2] {'seq'}, use_global_device_ids=true, to_apply=%region_15.16.clone | all-reduce | flops 32 | bytes 256
  (85 shorter events, 13.2 us)
Async XLA Ops:
  7.2 212.1 %copy-start = (bf16[1536,786]{0,1:T(8,128)(2,1)S(1)}, bf16[1536,786]{0,1:T(8,128)(2,1)}, u32[]{:S(2)}) copy-start(bf16[1536,786]{0,1:T(8,128)(2,1)} %param.29) | copy-start | bytes 7243780
  7.2 62.4 %all-gather.8.cloned.1.call-start = ((), (), s32[]{:S(2)}) async-start(), calls=%async_computation.3 | async-start | bytes 1671168 | tf_op jit(solution)/shard_map/all_gather | solution.py:21
  26.5 101.6 %reduce-scatter.5.cloned.1.call-start = ((), (), s32[]{:S(2)}) async-start(), calls=%async_computation.2 | async-start | bytes 1916928 | tf_op jit(solution)/shard_map/reduce_scatter | solution.py:204
  69.5 2.2 copy-start.1
  71.7 2.6 copy-start.7
  71.8 2.6 copy-start.8
  73.6 0.7 copy-start.2
  78.6 1.5 copy-start.9
  89.6 71.8 %copy-start.4 = (bf16[1,8,1536]{2,1,0:T(8,128)(2,1)S(1)}, bf16[1,8,1536]{2,1,0:T(8,128)(2,1)}, u32[]{:S(2)}) copy-start(bf16[1,8,1536]{2,1,0:T(8,128)(2,1)} %param.15) | copy-start | bytes 73732
  89.6 72.8 %copy-start.5 = (f32[1536]{0:T(1024)S(1)}, f32[1536]{0:T(1024)}, u32[]{:S(2)}) copy-start(f32[1536]{0:T(1024)} %param.28) | copy-start | bytes 18436
  89.6 84.5 %copy-start.10 = (s32[32]{0:T(128)S(1)}, s32[32]{0:T(128)}, u32[]{:S(2)}) copy-start(s32[32]{0:T(128)} %param.18) | copy-start | bytes 388
  89.6 86.5 %copy-start.6 = (s32[1,512]{1,0:T(1,128)S(1)}, s32[1,512]{1,0:T(1,128)}, u32[]{:S(2)}) copy-start(s32[1,512]{1,0:T(1,128)} %param.16) | copy-start | bytes 6148
  89.7 71.0 %reduce-scatter.7.cloned.1.call-start = ((), (), s32[]{:S(2)}) async-start(), calls=%async_computation.5 | async-start | bytes 266240
  128.2 91.1 %all-gather.10.cloned.1.call-start = ((), (), s32[]{:S(2)}) async-start(), calls=%async_computation.4 | async-start | bytes 1671168 | tf_op jit(solution)/shard_map/all_gather | solution.py:21
  162.4 59.7 %copy-start.3 = (bf16[8,1536]{1,0:T(8,128)(2,1)}, bf16[8,1536]{1,0:T(8,128)(2,1)S(1)}, u32[]{:S(2)}) copy-start(bf16[8,1536]{1,0:T(8,128)(2,1)S(1)} %get-tuple-element.32) | copy-start | bytes 73732
Sparse Core Ops, SparseCore 0:
  26.6 42.8 all-gather.7
  89.8 38.3 reduce-scatter.4
  131.0 29.6 reduce-scatter.6
  174.3 44.9 all-gather.9

commit v9 on v7

--- a/solution.py
+++ b/solution.py
@@ -17,7 +17,13 @@
 
 
 def gather_rows(rows):
-    part = lax.all_gather(rows, "bz", axis=0)
+    count = lax.axis_size("bz")
+    here = lax.axis_index("bz")
+    moved = [rows] + [
+        lax.ppermute(rows, "bz", [(i, (i + shift) % count) for i in range(count)])
+        for shift in range(1, count)
+    ]
+    part = jnp.take(jnp.stack(moved), (here - jnp.arange(count)) % count, axis=0)
     part = lax.all_gather(part, ("by", "bc"), axis=1)
     return part.reshape((-1,) + rows.shape[1:])
 

time: 272 us -> 281 us (1.033)
  blocking collectives: 81.9 us -> 46.2 us
  starting transfers between devices: 0.16 us -> 29.4 us
  waiting for transfers between devices: 136 us -> 150 us
    all_gather x2 -> x0, blocking collectives: 35.8 us -> none  [gather_rows(): part = lax.all_gather(rows, 'bz', axis=0)]
    ppermute x0 -> x6, starting transfers between devices: none -> 29.3 us  [gather_rows(): lax.ppermute(rows, 'bz', [(i, (i + shift) % count) for i in range(count)])]
    ppermute x0 -> x6, waiting for transfers between devices: none -> 9.25 us  [gather_rows(): lax.ppermute(rows, 'bz', [(i, (i + shift) % count) for i in range(count)])]
    all_gather x2, waiting for transfers between devices: 62 us -> 67.2 us  [gather_rows(): part = lax.all_gather(part, ('by', 'bc'), axis=1)]
  transfers between devices with their start and end apart: 4 -> 10, of which waited for: 4 -> 8; matrix products, arithmetic and copies ran while one was open for 5% -> 4% of each run, Pallas kernels for 0% -> 0%
where the time goes in v9:
time: 281 us
  waiting for transfers between devices  150 us (53%)
  blocking collectives  46.2 us (16%)
  starting transfers between devices  29.4 us (10%)
  other arithmetic  15.3 us (5%)
  between operations  15 us (5%)
  matrix products  13.1 us (5%)
  local copies, waits for them, and re-layouts  11.3 us (4%)
    all_gather x2, waiting for transfers between devices, gather_rows(): part = lax.all_gather(part, ('by', 'bc'), axis=1)  67.2 us
    reduce_scatter x1, waiting for transfers between devices, shards(): packed = lax.psum_scatter(packed, 'by', scatter_dimension=0)  42.8 us
    all_gather x2, blocking collectives, combine_blk(): pieces = lax.all_gather(jnp.stack([top, expsum, target]), axis, axis=0)  31.5 us
    unnamed x5, waiting for transfers between devices  31.1 us
    ppermute x6, starting transfers between devices, gather_rows(): lax.ppermute(rows, 'bz', [(i, (i + shift) % count) for i in range(count)])  29.3 us
    unnamed x1, blocking collectives  10.4 us
    ppermute x6, waiting for transfers between devices, gather_rows(): lax.ppermute(rows, 'bz', [(i, (i + shift) % count) for i in range(count)])  9.25 us
  transfers between devices with their start and end apart: 10, of which 8 were waited for; matrix products, arithmetic and copies ran while one was open for 4% of the time, Pallas kernels for 0%

profile of v9, /device:TPU:8, one launch (start us, length us, event | category | flops | bytes accessed | tf_op | source)
XLA Modules:
  0.0 280.6 jit_solution(15591971838661669326)
XLA Ops:
  7.3 11.1 %collective-permute-start.2 = (bf16[8,1536]{1,0:T(8,128)(2,1)}, bf16[8,1536]{1,0:T(8,128)(2,1)S(1)}, u32[]{:S(2)}, u32[]{:S(2)}) collective-permute-start(bf16[8,1536]{1,0:T(8,128)(2,1)} %bitcast.161), channel_id=1, source_target_pairs={{0,384},{128,0},{256,128},{384,256},{1,385},{129,1},{257,129},{385... | collective-permute-start | bytes 73736 | tf_op jit(solution)/shard_map/ppermute | solution.py:23
  18.3 1.9 collective-permute-start.1
  20.3 4.8 %collective-permute-start = (bf16[8,1536]{1,0:T(8,128)(2,1)}, bf16[8,1536]{1,0:T(8,128)(2,1)S(1)}, u32[]{:S(2)}, u32[]{:S(2)}) collective-permute-start(bf16[8,1536]{1,0:T(8,128)(2,1)} %bitcast.163), channel_id=1, source_target_pairs={{0,128},{128,256},{256,384},{384,0},{1,129},{129,257},{257,385},{3... | collective-permute-start | bytes 73736 | tf_op jit(solution)/shard_map/ppermute | solution.py:23
  25.2 3.4 %collective-permute-done.1 = bf16[8,1536]{1,0:T(8,128)(2,1)S(1)} collective-permute-done((bf16[8,1536]{1,0:T(8,128)(2,1)}, bf16[8,1536]{1,0:T(8,128)(2,1)S(1)}, u32[]{:S(2)}, u32[]{:S(2)}) %collective-permute-start.1) | collective-permute-done | bytes 24608 | tf_op jit(solution)/shard_map/ppermute | solution.py:23
  34.3 2.2 all_gather.33
  37.3 4.5 %compare_select_fusion.2 = s32[512,1]{0,1:T(1,128)S(1)} fusion(s32[]{:T(128)} %bitcast.15, s32[]{:T(128)} %bitcast.16, s32[]{:T(128)} %bitcast.17, s32[]{:T(128)} %bitcast.18, s32[]{:T(128)} %bitcast.19, s32[]{:T(128)} %bitcast.21, s32[]{:T(128)} %bitcast.20, s32[512,1]{0,1:T(1,128)S(1)} %bitcast.177, s32[512,1]{0,1:T(1,128)S(1)} %bitcast.175), kind=kLoop, calls=%fused_computation.106 | loop fusion | flops 7168 | bytes 6172 | tf_op jit(solution)/shard_map/jit(_take)/gather | solution.py:58
  43.0 30.2 %all-gather.9.cloned.1.call-done = bf16[4,128,1536]{2,1,0:T(8,128)(2,1)} async-done(((bf16[4,8,1536]{2,1,0:T(8,128)(2,1)}), bf16[4,128,1536]{2,1,0:T(8,128)(2,1)}) %all-gather.9.cloned.1.call-update) | async-done | bytes 1572880 | tf_op jit(solution)/shard_map/all_gather | solution.py:27
  73.3 2.1 convolution_convert_fusion.1
  75.5 1.9 convolution_convert_fusion
  79.3 1.6 divide_multiply_fusion
  86.6 2.0 all_gather.32
  90.9 2.4 concatenate.43
  93.4 42.8 %reduce-scatter.5.cloned.1.call-done = f32[1,4,8,1664]{3,2,1,0:T(8,128)} async-done(((f32[8,4,8,1664]{3,2,1,0:T(8,128)}), f32[1,4,8,1664]{3,2,1,0:T(8,128)}) %reduce-scatter.5.cloned.1.call-update) | async-done | bytes 213008 | tf_op jit(solution)/shard_map/reduce_scatter | solution.py:210
  136.2 31.0 %reduce-scatter.7.cloned.1.call-done = f32[1,8,1664]{2,1,0:T(8,128)} async-done(((f32[4,8,1664]{2,1,0:T(8,128)}), f32[1,8,1664]{2,1,0:T(8,128)}) %reduce-scatter.7.cloned.1.call-update) | async-done | bytes 53264
  169.2 4.3 %collective-permute-start.5 = (bf16[8,1536]{1,0:T(8,128)(2,1)S(1)}, bf16[8,1536]{1,0:T(8,128)(2,1)S(1)}, u32[]{:S(2)}, u32[]{:S(2)}) collective-permute-start(bf16[8,1536]{1,0:T(8,128)(2,1)S(1)} %fusion.41), channel_id=1, source_target_pairs={{0,384},{128,0},{256,128},{384,256},{1,385},{129,1},{257,129},{385... | collective-permute-start | bytes 73736 | tf_op jit(solution)/shard_map/ppermute | solution.py:23
  173.5 5.2 %collective-permute-start.4 = (bf16[8,1536]{1,0:T(8,128)(2,1)S(1)}, bf16[8,1536]{1,0:T(8,128)(2,1)S(1)}, u32[]{:S(2)}, u32[]{:S(2)}) collective-permute-start(bf16[8,1536]{1,0:T(8,128)(2,1)S(1)} %fusion.41), channel_id=1, source_target_pairs={{0,256},{128,384},{256,0},{384,128},{1,257},{129,385},{257,1},{385... | collective-permute-start | bytes 73736 | tf_op jit(solution)/shard_map/ppermute | solution.py:23
  178.7 1.9 collective-permute-start.3
  180.7 2.4 collective-permute-done.4
  183.1 3.4 %collective-permute-done.3 = bf16[8,1536]{1,0:T(8,128)(2,1)S(1)} collective-permute-done((bf16[8,1536]{1,0:T(8,128)(2,1)S(1)}, bf16[8,1536]{1,0:T(8,128)(2,1)S(1)}, u32[]{:S(2)}, u32[]{:S(2)}) %collective-permute-start.3) | collective-permute-done | bytes 24608 | tf_op jit(solution)/shard_map/ppermute | solution.py:23
  189.9 37.0 %all-gather.11.cloned.1.call-done = bf16[4,128,1536]{2,1,0:T(8,128)(2,1)} async-done(((bf16[4,8,1536]{2,1,0:T(8,128)(2,1)}), bf16[4,128,1536]{2,1,0:T(8,128)(2,1)}) %all-gather.11.cloned.1.call-update) | async-done | bytes 1572880 | tf_op jit(solution)/shard_map/all_gather | solution.py:27
  226.9 2.9 %fusion.77 = (f32[512]{0:T(512)S(1)}, f32[512,786]{0,1:T(8,128)S(1)}) fusion(bf16[512,1536]{1,0:T(8,128)(2,1)} %bitcast.200, bf16[1536,786]{0,1:T(8,128)(2,1)S(1)} %copy-done), kind=kOutput, calls=%fused_computation.179 | convolution fusion | flops 1236673024 | bytes 5599232 | tf_op jit(solution)/shard_map/dot_general | solution.py:215
  230.3 15.3 %all-gather.4 = f32[16,3,512]{2,1,0:T(4,128)S(1)} all-gather(f32[1,3,512]{2,1,0:T(4,128)S(1)} %maximum_bitcast_fusion), channel_id=4, replica_groups=mesh['bz'=4,'by'=8,'bc'=2,'seq'=4,'mp'=2] {'by','bc'}, dimensions={0}, use_global_device_ids=true | all-gather | bytes 104448 | tf_op jit(solution)/shard_map/all_gather | solution.py:47
  245.7 16.3 %all-gather.5 = f32[4,3,512]{2,1,0:T(4,128)S(1)} all-gather(f32[1,3,512]{2,1,0:T(4,128)S(1)} %maximum_bitcast_fusion.1), channel_id=5, replica_groups=mesh['bz'=4,'by'=8,'bc'=2,'seq'=4,'mp'=2] {'bz'}, dimensions={0}, use_global_device_ids=true | all-gather | bytes 30720 | tf_op jit(solution)/shard_map/all_gather | solution.py:47
  263.1 10.4 %all-reduce.7 = f32[32]{0:T(128)S(1)} all-reduce(f32[32]{0:T(128)S(1)} %convolution_bitcast_fusion.1), channel_id=8, replica_groups=mesh['bz'=4,'by'=8,'bc'=2,'seq'=4,'mp'=2] {'seq'}, use_global_device_ids=true, to_apply=%region_18.20.clone | all-reduce | flops 32 | bytes 256
  (116 shorter events, 24.6 us)
Async XLA Ops:
  7.2 219.8 %copy-start = (bf16[1536,786]{0,1:T(8,128)(2,1)S(1)}, bf16[1536,786]{0,1:T(8,128)(2,1)}, u32[]{:S(2)}) copy-start(bf16[1536,786]{0,1:T(8,128)(2,1)} %param.31) | copy-start | bytes 7243780
  7.2 29.3 %copy-start.12 = (s32[1,8]{1,0:T(1,128)S(1)}, s32[1,8]{1,0:T(1,128)}, u32[]{:S(2)}) copy-start(s32[1,8]{1,0:T(1,128)} %param.19) | copy-start | bytes 100
  7.2 30.0 %copy-start.8 = (f32[4,48]{1,0:T(4,128)S(1)}, f32[4,48]{1,0:T(4,128)}, u32[]{:S(2)}) copy-start(f32[4,48]{1,0:T(4,128)} %param.23) | copy-start | bytes 2308
  7.2 35.8 %copy-start.7 = (f32[4,256]{1,0:T(4,128)S(1)}, f32[4,256]{1,0:T(4,128)}, u32[]{:S(2)}) copy-start(f32[4,256]{1,0:T(4,128)} %param.24) | copy-start | bytes 12292
  7.2 66.1 %copy-start.3 = (bf16[1536,2,48]{0,2,1:T(8,128)(2,1)S(1)}, bf16[1536,2,48]{0,2,1:T(8,128)(2,1)}, u32[]{:S(2)}) copy-start(bf16[1536,2,48]{0,2,1:T(8,128)(2,1)} %param.21) | copy-start | bytes 884740
  7.2 66.0 %all-gather.9.cloned.1.call-start = ((), (), s32[]{:S(2)}) async-start(), calls=%async_computation.3 | async-start | bytes 1671168 | tf_op jit(solution)/shard_map/all_gather | solution.py:27
  7.3 17.9 %collective-permute-start.2 = (bf16[8,1536]{1,0:T(8,128)(2,1)}, bf16[8,1536]{1,0:T(8,128)(2,1)S(1)}, u32[]{:S(2)}, u32[]{:S(2)}) collective-permute-start(bf16[8,1536]{1,0:T(8,128)(2,1)} %bitcast.161), channel_id=1, source_target_pairs={{0,384},{128,0},{256,128},{384,256},{1,385},{129,1},{257,129},{385... | collective-permute-start | bytes 73736 | tf_op jit(solution)/shard_map/ppermute | solution.py:23
  18.3 10.2 %collective-permute-start.1 = (bf16[8,1536]{1,0:T(8,128)(2,1)}, bf16[8,1536]{1,0:T(8,128)(2,1)S(1)}, u32[]{:S(2)}, u32[]{:S(2)}) collective-permute-start(bf16[8,1536]{1,0:T(8,128)(2,1)} %bitcast.162), channel_id=1, source_target_pairs={{0,256},{128,384},{256,0},{384,128},{1,257},{129,385},{257,1},{385... | collective-permute-start | bytes 73736 | tf_op jit(solution)/shard_map/ppermute | solution.py:23
  20.3 8.3 %collective-permute-start = (bf16[8,1536]{1,0:T(8,128)(2,1)}, bf16[8,1536]{1,0:T(8,128)(2,1)S(1)}, u32[]{:S(2)}, u32[]{:S(2)}) collective-permute-start(bf16[8,1536]{1,0:T(8,128)(2,1)} %bitcast.163), channel_id=1, source_target_pairs={{0,128},{128,256},{256,384},{384,0},{1,129},{129,257},{257,385},{3... | collective-permute-start | bytes 73736 | tf_op jit(solution)/shard_map/ppermute | solution.py:23
  30.6 105.5 %reduce-scatter.5.cloned.1.call-start = ((), (), s32[]{:S(2)}) async-start(), calls=%async_computation.2 | async-start | bytes 1916928 | tf_op jit(solution)/shard_map/reduce_scatter | solution.py:210
  73.3 2.2 copy-start.1
  75.4 2.6 copy-start.10
  75.4 2.6 copy-start.11
  82.3 1.5 copy-start.13
  93.3 74.8 %copy-start.5 = (bf16[1,8,1536]{2,1,0:T(8,128)(2,1)S(1)}, bf16[1,8,1536]{2,1,0:T(8,128)(2,1)}, u32[]{:S(2)}) copy-start(bf16[1,8,1536]{2,1,0:T(8,128)(2,1)} %param.17) | copy-start | bytes 73732
  93.3 75.8 %copy-start.6 = (f32[1536]{0:T(1024)S(1)}, f32[1536]{0:T(1024)}, u32[]{:S(2)}) copy-start(f32[1536]{0:T(1024)} %param.30) | copy-start | bytes 18436
  93.3 94.6 %copy-start.14 = (s32[32]{0:T(128)S(1)}, s32[32]{0:T(128)}, u32[]{:S(2)}) copy-start(s32[32]{0:T(128)} %param.20) | copy-start | bytes 388
  93.3 96.6 %copy-start.9 = (s32[1,512]{1,0:T(1,128)S(1)}, s32[1,512]{1,0:T(1,128)}, u32[]{:S(2)}) copy-start(s32[1,512]{1,0:T(1,128)} %param.18) | copy-start | bytes 6148
  93.3 73.9 %reduce-scatter.7.cloned.1.call-start = ((), (), s32[]{:S(2)}) async-start(), calls=%async_computation.5 | async-start | bytes 266240
  136.2 90.7 %all-gather.11.cloned.1.call-start = ((), (), s32[]{:S(2)}) async-start(), calls=%async_computation.4 | async-start | bytes 1671168 | tf_op jit(solution)/shard_map/all_gather | solution.py:27
  169.1 60.8 %copy-start.4 = (bf16[8,1536]{1,0:T(8,128)(2,1)}, bf16[8,1536]{1,0:T(8,128)(2,1)S(1)}, u32[]{:S(2)}) copy-start(bf16[8,1536]{1,0:T(8,128)(2,1)S(1)} %get-tuple-element.35) | copy-start | bytes 73732
  169.2 11.6 %collective-permute-start.5 = (bf16[8,1536]{1,0:T(8,128)(2,1)S(1)}, bf16[8,1536]{1,0:T(8,128)(2,1)S(1)}, u32[]{:S(2)}, u32[]{:S(2)}) collective-permute-start(bf16[8,1536]{1,0:T(8,128)(2,1)S(1)} %fusion.41), channel_id=1, source_target_pairs={{0,384},{128,0},{256,128},{384,256},{1,385},{129,1},{257,129},{385... | collective-permute-start | bytes 73736 | tf_op jit(solution)/shard_map/ppermute | solution.py:23
  173.5 9.6 %collective-permute-start.4 = (bf16[8,1536]{1,0:T(8,128)(2,1)S(1)}, bf16[8,1536]{1,0:T(8,128)(2,1)S(1)}, u32[]{:S(2)}, u32[]{:S(2)}) collective-permute-start(bf16[8,1536]{1,0:T(8,128)(2,1)S(1)} %fusion.41), channel_id=1, source_target_pairs={{0,256},{128,384},{256,0},{384,128},{1,257},{129,385},{257,1},{385... | collective-permute-start | bytes 73736 | tf_op jit(solution)/shard_map/ppermute | solution.py:23
  178.7 7.8 %collective-permute-start.3 = (bf16[8,1536]{1,0:T(8,128)(2,1)S(1)}, bf16[8,1536]{1,0:T(8,128)(2,1)S(1)}, u32[]{:S(2)}, u32[]{:S(2)}) collective-permute-start(bf16[8,1536]{1,0:T(8,128)(2,1)S(1)} %fusion.41), channel_id=1, source_target_pairs={{0,128},{128,256},{256,384},{384,0},{1,129},{129,257},{257,385},{3... | collective-permute-start | bytes 73736 | tf_op jit(solution)/shard_map/ppermute | solution.py:23
  (1 other events, 0.7 us)
Sparse Core Ops, SparseCore 0:
  30.8 42.4 all-gather.8
  93.5 42.6 reduce-scatter.4
  139.0 28.2 reduce-scatter.6
  188.0 38.8 all-gather.10

commit v10 on v7

--- a/solution.py
+++ b/solution.py
@@ -34,6 +34,12 @@
 
 def sum_blk(values):
     return lax.psum(lax.psum(lax.psum(values, "bc"), "by"), "bz")
+
+
+def merge_pieces(pieces):
+    top = jnp.max(pieces[:, 0], axis=0)
+    expsum = jnp.sum(pieces[:, 1] * jnp.exp(pieces[:, 0] - top[None]), axis=0)
+    return top, expsum, jnp.sum(pieces[:, 2], axis=0)
 
 
 def combine_blk(top, expsum, target):
@@ -217,21 +223,27 @@
     target_local = jnp.sum(jnp.where(hit, logits, 0.0), axis=1)
     top_local = jnp.max(logits, axis=1)
     expsum_local = jnp.sum(jnp.exp(logits - top_local[:, None]), axis=1)
-    top_all, expsum_all, target_all = combine_blk(top_local, expsum_local, target_local)
-    logprob = target_all - (top_all + jnp.log(expsum_all))
+    top, expsum, target = merge_pieces(
+        lax.all_gather(jnp.stack([top_local, expsum_local, target_local]), ("by", "bc"), axis=0)
+    )
+    seqs_count = lengths.shape[1]
+    groups = lax.axis_size("seq")
+    seq_index = lax.axis_index("seq")
+    payload = jnp.stack([top, expsum, target, segment.astype(jnp.float32)])
+    every = lax.all_gather(payload, ("bz", "seq"), axis=0)
+    every = every.reshape(lax.axis_size("bz"), groups, 4, tokens_all)
+    top_g, expsum_g, target_g = merge_pieces(jnp.moveaxis(every[:, :, :3], 2, 1))
+    segment_g = every[0, :, 3]
+    logprob_g = target_g - (top_g + jnp.log(expsum_g))
+    logprob = lax.dynamic_index_in_dim(logprob_g, seq_index, axis=0, keepdims=False)
     token_own = lax.dynamic_slice_in_dim(logprob, blk_index * rows_count, rows_count, 0)
-    seqs_count = lengths.shape[1]
-    onehot = (segment[:, None] == jnp.arange(seqs_count, dtype=jnp.int32)[None, :]).astype(
-        jnp.float32
-    )
-    sums = jnp.dot(logprob, onehot, precision=HIGH)
-    seq_index = lax.axis_index("seq")
-    mine = lax.dynamic_slice_in_dim(owners, seq_index * seqs_count, seqs_count, 0)
-    placement = (mine[:, None] == jnp.arange(owners.shape[0], dtype=jnp.int32)[None, :]).astype(
-        jnp.float32
-    )
-    spread_sums = jnp.dot(sums, placement, precision=HIGH)
-    seq_own = lax.psum_scatter(spread_sums, "seq", scatter_dimension=0, tiled=True)
+    onehot = (
+        segment_g[:, :, None] == jnp.arange(seqs_count, dtype=jnp.float32)[None, None, :]
+    ).astype(jnp.float32)
+    sums = jnp.einsum("gt,gtk->gk", logprob_g, onehot, precision=HIGH).reshape(-1)
+    slots = seq_index * seqs_count + jnp.arange(seqs_count, dtype=jnp.int32)
+    placement = (owners[:, None] == slots[None, :]).astype(jnp.float32)
+    seq_own = jnp.dot(sums, placement, precision=HIGH)
     return (layer_own[None], token_own[None], seq_own)
 
 

time: 272 us -> 291 us (1.070)
  the two profiles are of different devices: /device:TPU:8 before, /device:TPU:16 now
where the time goes in v10:
time: 291 us; the launch traced here: 290 us
  waiting for transfers between devices  137 us (47%)
  blocking collectives  101 us (35%)
  between operations  14.2 us (5%)
  matrix products  14 us (5%)
  other arithmetic  13.7 us (5%)
  local copies, waits for them, and re-layouts  10 us (3%)
    all_gather x2, waiting for transfers between devices, gather_rows(): part = lax.all_gather(part, ('by', 'bc'), axis=1)  61.9 us
    all_gather x1, blocking collectives, shards(): every = lax.all_gather(payload, ('bz', 'seq'), axis=0)  45.4 us
    reduce_scatter x1, waiting for transfers between devices, shards(): packed = lax.psum_scatter(packed, 'by', scatter_dimension=0)  42.6 us
    all_gather x2, blocking collectives, gather_rows(): part = lax.all_gather(rows, 'bz', axis=0)  35.8 us
    unnamed x5, waiting for transfers between devices  32.5 us
    all_gather x1, blocking collectives, shards(): lax.all_gather(jnp.stack([top_local, expsum_local, target_local]), ('by',...  16 us
  transfers between devices with their start and end apart: 4, of which 4 were waited for; matrix products, arithmetic and copies ran while one was open for 4% of the time, Pallas kernels for 0%

profile of v10, /device:TPU:16, one launch (start us, length us, event | category | flops | bytes accessed | tf_op | source)
XLA Modules:
  0.0 290.5 jit_solution(15739814355257954256)
XLA Ops:
  7.2 21.3 %all_gather.39 = bf16[4,8,1536]{2,1,0:T(8,128)(2,1)} all-gather(bf16[1,8,1536]{2,1,0:T(8,128)(2,1)} %param.15), channel_id=1, replica_groups=mesh['bz'=4,'by'=8,'bc'=2,'seq'=4,'mp'=2] {'bz'}, dimensions={0}, use_global_device_ids=true | all-gather | bytes 122880 | tf_op jit(solution)/shard_map/all_gather | solution.py:20
  30.8 1.4 gather_fusion
  32.2 2.2 all_gather.43
  36.7 4.5 %compare_select_fusion.2 = s32[512,1]{0,1:T(1,128)S(1)} fusion(s32[]{:T(128)} %bitcast.12, s32[]{:T(128)} %bitcast.13, s32[]{:T(128)} %bitcast.14, s32[]{:T(128)} %bitcast.15, s32[]{:T(128)} %bitcast.16, s32[]{:T(128)} %bitcast.18, s32[]{:T(128)} %bitcast.17, s32[512,1]{0,1:T(1,128)S(1)} %bitcast.167, s32[512,1]{0,1:T(1,128)S(1)} %bitcast.165), kind=kLoop, calls=%fused_computation.107 | loop fusion | flops 7168 | bytes 6172 | tf_op jit(solution)/shard_map/jit(_take)/gather | solution.py:58
  41.1 1.3 compare_convert_fusion.4
  42.4 0.8 fusion.81
  43.3 23.6 %all-gather.10.cloned.1.call-done = bf16[4,128,1536]{2,1,0:T(8,128)(2,1)} async-done(((bf16[4,8,1536]{2,1,0:T(8,128)(2,1)}), bf16[4,128,1536]{2,1,0:T(8,128)(2,1)}) %all-gather.10.cloned.1.call-update) | async-done | bytes 1572880 | tf_op jit(solution)/shard_map/all_gather | solution.py:21
  66.9 2.2 convolution_convert_fusion.1
  69.1 1.9 convolution_convert_fusion
  73.0 1.6 divide_multiply_fusion
  74.6 1.0 fusion.31
  75.9 1.5 fusion.8
  77.4 1.5 multiply_convert_fusion
  80.2 2.0 all_gather.42
  83.0 1.5 fusion.29
  84.5 2.4 concatenate.43
  87.0 42.6 %reduce-scatter.5.cloned.1.call-done = f32[1,4,8,1664]{3,2,1,0:T(8,128)} async-done(((f32[8,4,8,1664]{3,2,1,0:T(8,128)}), f32[1,4,8,1664]{3,2,1,0:T(8,128)}) %reduce-scatter.5.cloned.1.call-update) | async-done | bytes 213008 | tf_op jit(solution)/shard_map/reduce_scatter | solution.py:210
  129.7 32.4 %reduce-scatter.7.cloned.1.call-done = f32[1,8,1664]{2,1,0:T(8,128)} async-done(((f32[4,8,1664]{2,1,0:T(8,128)}), f32[1,8,1664]{2,1,0:T(8,128)}) %reduce-scatter.7.cloned.1.call-update) | async-done | bytes 53264
  162.9 1.0 fusion.40
  164.0 14.5 %all-gather.1 = bf16[32,1536]{1,0:T(8,128)(2,1)} all-gather(bf16[8,1536]{1,0:T(8,128)(2,1)S(1)} %fusion.42), channel_id=3, replica_groups=mesh['bz'=4,'by'=8,'bc'=2,'seq'=4,'mp'=2] {'bz'}, dimensions={0}, use_global_device_ids=true | all-gather | bytes 122880 | tf_op jit(solution)/shard_map/all_gather | solution.py:20
  178.5 38.3 %all-gather.12.cloned.1.call-done = bf16[4,128,1536]{2,1,0:T(8,128)(2,1)} async-done(((bf16[4,8,1536]{2,1,0:T(8,128)(2,1)}), bf16[4,128,1536]{2,1,0:T(8,128)(2,1)}) %all-gather.12.cloned.1.call-update) | async-done | bytes 1572880 | tf_op jit(solution)/shard_map/all_gather | solution.py:21
  216.8 2.9 fusion.83
  220.2 16.0 %all-gather.5 = f32[16,3,512]{2,1,0:T(4,128)S(1)} all-gather(f32[1,3,512]{2,1,0:T(4,128)S(1)} %maximum_bitcast_fusion), channel_id=5, replica_groups=mesh['bz'=4,'by'=8,'bc'=2,'seq'=4,'mp'=2] {'by','bc'}, dimensions={0}, use_global_device_ids=true | all-gather | bytes 104448 | tf_op jit(solution)/shard_map/all_gather | solution.py:227
  236.3 45.4 %all-gather.6 = f32[16,4,512]{2,1,0:T(4,128)S(1)} all-gather(f32[1,4,512]{2,1,0:T(4,128)S(1)} %maximum_bitcast_fusion.1), channel_id=6, replica_groups=mesh['bz'=4,'by'=8,'bc'=2,'seq'=4,'mp'=2] {'bz','seq'}, dimensions={0}, use_global_device_ids=true | all-gather | bytes 139264 | tf_op jit(solution)/shard_map/all_gather | solution.py:233
  (90 shorter events, 12.6 us)
Async XLA Ops:
  7.2 209.6 %copy-start = (bf16[1536,786]{0,1:T(8,128)(2,1)S(1)}, bf16[1536,786]{0,1:T(8,128)(2,1)}, u32[]{:S(2)}) copy-start(bf16[1536,786]{0,1:T(8,128)(2,1)} %param.29) | copy-start | bytes 7243780
  7.2 59.7 %all-gather.10.cloned.1.call-start = ((), (), s32[]{:S(2)}) async-start(), calls=%async_computation.3 | async-start | bytes 1671168 | tf_op jit(solution)/shard_map/all_gather | solution.py:21
  28.6 101.0 %reduce-scatter.5.cloned.1.call-start = ((), (), s32[]{:S(2)}) async-start(), calls=%async_computation.2 | async-start | bytes 1916928 | tf_op jit(solution)/shard_map/reduce_scatter | solution.py:210
  66.9 2.2 copy-start.1
  69.1 2.6 copy-start.7
  69.1 2.6 copy-start.8
  71.0 0.7 copy-start.2
  75.9 1.5 copy-start.9
  86.9 76.0 %copy-start.4 = (bf16[1,8,1536]{2,1,0:T(8,128)(2,1)S(1)}, bf16[1,8,1536]{2,1,0:T(8,128)(2,1)}, u32[]{:S(2)}) copy-start(bf16[1,8,1536]{2,1,0:T(8,128)(2,1)} %param.15) | copy-start | bytes 73732
  86.9 77.0 %copy-start.5 = (f32[1536]{0:T(1024)S(1)}, f32[1536]{0:T(1024)}, u32[]{:S(2)}) copy-start(f32[1536]{0:T(1024)} %param.28) | copy-start | bytes 18436
  86.9 91.6 %copy-start.6 = (s32[1,512]{1,0:T(1,128)S(1)}, s32[1,512]{1,0:T(1,128)}, u32[]{:S(2)}) copy-start(s32[1,512]{1,0:T(1,128)} %param.16) | copy-start | bytes 6148
  87.0 75.1 %reduce-scatter.7.cloned.1.call-start = ((), (), s32[]{:S(2)}) async-start(), calls=%async_computation.5 | async-start | bytes 266240
  129.6 87.2 %all-gather.12.cloned.1.call-start = ((), (), s32[]{:S(2)}) async-start(), calls=%async_computation.4 | async-start | bytes 1671168 | tf_op jit(solution)/shard_map/all_gather | solution.py:21
  163.9 55.8 %copy-start.3 = (bf16[8,1536]{1,0:T(8,128)(2,1)}, bf16[8,1536]{1,0:T(8,128)(2,1)S(1)}, u32[]{:S(2)}) copy-start(bf16[8,1536]{1,0:T(8,128)(2,1)S(1)} %get-tuple-element.34) | copy-start | bytes 73732
  219.7 63.5 %copy-start.10 = (s32[32]{0:T(128)S(1)}, s32[32]{0:T(128)}, u32[]{:S(2)}) copy-start(s32[32]{0:T(128)} %param.18) | copy-start | bytes 388
Sparse Core Ops, SparseCore 0:
  28.7 38.1 all-gather.9
  87.1 42.4 reduce-scatter.4
  132.4 29.6 reduce-scatter.6
  178.6 38.1 all-gather.11
